TPU v7x, 512 devices: a whole 4x8x8 slice. The times are simulated.
512 devices in a mesh: grp: 8 (over y_hi, core), cp: 64 (over y_lo, x, z).
Axes of the slice: x: 4, y: 8 (y_hi: 4, y_lo: 2; y = y_hi * 2 + y_lo), z: 8, core: 2. Of those that a mesh axis runs over, the one named last changes fastest.
Arguments:
- query_long: bfloat16 [8, 32768, 1024], P('grp', 'cp'), may hold values from -20 to 20
- long_prompt_keys: bfloat16 [8, 32768, 512], P('grp', 'cp'), may hold values from -11 to 11
- long_prompt_values: bfloat16 [8, 32768, 512], P('grp', 'cp'), may hold values from -6 to 6
- long_length: int32 [8, 8], P('grp'), may hold values from 2048 to 4096, as said below
- short_prompt_queries: bfloat16 [8, 8192, 1024], P('grp', 'cp'), may hold values from -20 to 20
- short_prompt_keys: bfloat16 [8, 8192, 512], P('grp', 'cp'), may hold values from -11 to 11
- short_prompt_values: bfloat16 [8, 8192, 512], P('grp', 'cp'), may hold values from -6 to 6
- short_prompt_index: int32 [8, 64, 128], P('grp', 'cp'), may hold values from 0 to 3, never falling along the last dimension, each value on 1 to 64 neighbouring positions
- page_owner: int32 [8, 256], P('grp', 'cp'), may hold values from 0 to 7, as said below
- page_slot: int32 [8, 256], P('grp', 'cp'), may hold values from 0 to 3, as said below
Outputs:
- long_attention: bfloat16 [8, 32768, 1024], P('grp', 'cp')
- short_attention: bfloat16 [8, 8192, 1024], P('grp', 'cp')
- page_cache: bfloat16 [8, 256, 128, 1024], P('grp', 'cp')
Inputs may be any that keep to these rules, and one draw needn't show every extreme that they name: `long_length`: each long prompt has from half of 4096 to 4096 tokens, and some prompt has exactly 4096. `page_owner`: page k of the device at grp index g and cp index c goes to grp index (g + an offset that depends on c and k) modulo the number of grp devices, at the same cp index. A device sends at most 1 of its pages to one owner, and exactly 1 to some owners. Every device receives exactly 4 pages. `page_slot`: the pages that reach one device take each of its slots once.
All inputs are finite; a program needn't handle non-finite values.
Results may differ from a plain program's by a relative error of at most 0.0055.
Values may be sent and summed in bfloat16 or wider, within the bound.
No kernel may reach another device: no remote copies, remote signals or barrier semaphores. Data moves between devices by JAX's collectives and lax.ppermute only.
A program may use at most 128 MiB of HBM per device.

v0:
```python
import math

import jax
import jax.numpy as jnp
from jax import lax
from jax.sharding import PartitionSpec as P

QUERY_HEADS = 8
KEY_VALUE_HEADS = 4
HEAD_SIZE = 128
PAGE = 128
SPAN = 8


def shifted(x, axis, by):
    size = lax.axis_size(axis)
    pairs = [(i, i + by) for i in range(size) if 0 <= i + by < size]
    return lax.ppermute(x, axis, pairs)


def head_scores(query_rows, key_row_block, visible):
    paired_count, count_of_rows = (query_rows.shape[0], query_rows.shape[1])
    grouped_heads = query_rows.reshape(
        paired_count, count_of_rows, KEY_VALUE_HEADS, QUERY_HEADS // KEY_VALUE_HEADS, HEAD_SIZE
    )
    key_head_rows = key_row_block.reshape(
        paired_count, key_row_block.shape[1], KEY_VALUE_HEADS, HEAD_SIZE
    )
    scores = jnp.einsum(
        "prgjd,pkgd->pgjrk", grouped_heads, key_head_rows, preferred_element_type=jnp.float32
    )
    scores = scores / math.sqrt(HEAD_SIZE)
    return jnp.where(visible[:, None, None], scores, -jnp.inf)


def block_stats(query_rows, key_row_block, value_row_block, visible):
    scores = head_scores(query_rows, key_row_block, visible)
    highest = jnp.max(scores, axis=-1)
    anchor = jnp.where(jnp.isfinite(highest), highest, 0.0)
    weights = jnp.where(visible[:, None, None], jnp.exp(scores - anchor[..., None]), 0.0)
    weight_sum = jnp.sum(weights, axis=-1)
    value_head_rows = value_row_block.reshape(
        value_row_block.shape[0], value_row_block.shape[1], KEY_VALUE_HEADS, HEAD_SIZE
    )
    summed = jnp.einsum(
        "pgjrk,pkgd->pgjrd",
        weights.astype(jnp.bfloat16),
        value_head_rows,
        preferred_element_type=jnp.float32,
    )
    return (highest, weight_sum, summed)


def merge_stats(former, latter):
    top_one, sum_one, acc_one = former
    top_two, sum_two, acc_two = latter
    highest = jnp.maximum(top_one, top_two)
    anchor = jnp.where(jnp.isfinite(highest), highest, 0.0)
    scale_one = jnp.exp(top_one - anchor)
    scale_two = jnp.exp(top_two - anchor)
    return (
        highest,
        scale_one * sum_one + scale_two * sum_two,
        scale_one[..., None] * acc_one + scale_two[..., None] * acc_two,
    )


def select_stats(condition, chosen, other):
    return jax.tree.map(
        lambda left_leaf, right_leaf: jnp.where(condition, left_leaf, right_leaf), chosen, other
    )


def take_pair(pair_stats, position_in):
    return jax.tree.map(lambda leaf_array: leaf_array[position_in], pair_stats)


def finish_rows(stats_in, live_rows):
    highest, weight_sum, summed = stats_in
    divisor = jnp.where(weight_sum > 0, weight_sum, 1.0)
    result = summed / divisor[..., None]
    result = jnp.where(live_rows[None, None, :, None], result, 0.0)
    return jnp.transpose(result, (2, 0, 1, 3)).reshape(live_rows.shape[0], QUERY_HEADS * HEAD_SIZE)


def long_visible(query_pos, key_pos, length):
    return (key_pos[:, None, :] <= query_pos[:, :, None]) & (key_pos[:, None, :] < length)


def per_device(
    query_long,
    long_prompt_keys,
    long_prompt_values,
    long_length,
    short_prompt_queries,
    short_prompt_keys,
    short_prompt_values,
    short_prompt_index,
    page_owner,
    page_slot,
):
    half_rows = query_long.shape[1] // 2
    stride = lax.axis_size("cp") // SPAN
    device_cp = lax.axis_index("cp")
    member = device_cp // stride
    group_id = device_cp % stride
    length = lax.dynamic_index_in_dim(long_length[0], group_id, 0, keepdims=False)
    offsets = jnp.arange(half_rows, dtype=jnp.int32)

    def block_positions(block_id):
        return block_id * half_rows + offsets

    pos_first = block_positions(member)
    pos_second = block_positions(2 * SPAN - 1 - member)
    query_first = query_long[0, :half_rows]
    query_second = query_long[0, half_rows:]
    key_row_block = long_prompt_keys[0]
    value_row_block = long_prompt_values[0]
    key_first, key_second = (key_row_block[:half_rows], key_row_block[half_rows:])
    value_first, value_second = (value_row_block[:half_rows], value_row_block[half_rows:])
    upper_gate = jnp.array(True)
    self_stats = block_stats(
        jnp.stack([query_first, query_second, query_second]),
        jnp.stack([key_first, key_first, key_second]),
        jnp.stack([value_first, value_first, value_second]),
        long_visible(
            jnp.stack([pos_first, pos_second, pos_second]),
            jnp.stack([pos_first, pos_first, pos_second]),
            length,
        ),
    )
    first_state = take_pair(self_stats, 0)
    second_state = merge_stats(take_pair(self_stats, 1), take_pair(self_stats, 2))

    def absorb(states, source, source_keys, source_values):
        state_first, state_second = states
        below_self = source < member
        src_first = block_positions(source)
        src_second = block_positions(2 * SPAN - 1 - source)
        key_lead, key_tail = source_keys
        value_lead, value_tail = source_values
        query_rows = jnp.stack([jnp.where(below_self, query_first, query_second), query_second])
        query_pos = jnp.stack([jnp.where(below_self, pos_first, pos_second), pos_second])
        keys_pair = jnp.stack([key_lead, jnp.where(below_self, key_lead, key_tail)])
        values_pair = jnp.stack([value_lead, jnp.where(below_self, value_lead, value_tail)])
        key_pos = jnp.stack([src_first, jnp.where(below_self, src_first, src_second)])
        pair_stats = block_stats(
            query_rows, keys_pair, values_pair, long_visible(query_pos, key_pos, length)
        )
        part_one = take_pair(pair_stats, 0)
        part_two = take_pair(pair_stats, 1)
        lower_first = merge_stats(state_first, part_one)
        lower_second = merge_stats(state_second, part_two)
        upper_second = merge_stats(merge_stats(state_second, part_one), part_two)
        return (
            select_stats(below_self, lower_first, state_first),
            select_stats(below_self, lower_second, upper_second),
        )

    def advance(step_id, loop_carry):
        states, keys_up, values_up, keys_down, values_down = loop_carry
        keys_up, values_up = shifted((keys_up, values_up), "cp", stride)
        keys_down, values_down = shifted((keys_down, values_down), "cp", -stride)
        below_id = member - step_id
        above_id = member + step_id
        states = lax.cond(
            below_id >= 0,
            lambda: absorb(states, below_id, (keys_up, keys_up), (values_up, values_up)),
            lambda: states,
        )
        states = lax.cond(
            (above_id < SPAN) & upper_gate,
            lambda: absorb(
                states,
                above_id,
                (keys_down[:half_rows], keys_down[half_rows:]),
                (values_down[:half_rows], values_down[half_rows:]),
            ),
            lambda: states,
        )
        return (states, keys_up, values_up, keys_down, values_down)

    loop_result = lax.fori_loop(
        1,
        SPAN,
        advance,
        ((first_state, second_state), key_first, value_first, key_row_block, value_row_block),
    )
    first_state, second_state = loop_result[0]
    long_out = jnp.concatenate(
        [
            finish_rows(first_state, pos_first < length),
            finish_rows(second_state, pos_second < length),
        ],
        axis=0,
    )
    segment_row = short_prompt_index[0, 0]
    order_ids = jnp.arange(segment_row.shape[0], dtype=jnp.int32)
    short_visible = (order_ids[None, :] <= order_ids[:, None]) & (
        segment_row[None, :] == segment_row[:, None]
    )
    short_stats = block_stats(
        short_prompt_queries[0][None],
        short_prompt_keys[0][None],
        short_prompt_values[0][None],
        short_visible[None],
    )
    short_prompt_output = finish_rows(take_pair(short_stats, 0), order_ids >= 0)
    kv_rows = jnp.concatenate([key_row_block, value_row_block], axis=-1)
    row_positions = jnp.concatenate([pos_first, pos_second])
    kv_rows = jnp.where((row_positions < length)[:, None], kv_rows, jnp.zeros_like(kv_rows))
    page_count = kv_rows.shape[0] // PAGE
    page_width = kv_rows.shape[1]
    page_data = kv_rows.reshape(page_count, PAGE * page_width)
    owners = page_owner[0]
    slot_ids = page_slot[0]
    groups = lax.axis_size("grp")
    capacity = max(1, page_count // groups)
    page_ids = jnp.arange(page_count, dtype=jnp.int32)
    earlier = jnp.sum(
        (owners[None, :] == owners[:, None]) & (page_ids[None, :] < page_ids[:, None]), axis=1
    )
    target = owners * capacity + earlier
    bucket_ids = jnp.arange(groups * capacity, dtype=jnp.int32)
    onehot = target[None, :] == bucket_ids[:, None]
    outgoing = jnp.dot(
        onehot.astype(jnp.bfloat16), page_data, preferred_element_type=jnp.float32
    ).astype(jnp.bfloat16)
    out_slots = jnp.max(jnp.where(onehot, slot_ids[None, :], -1), axis=1)
    incoming, in_slots = (
        lax.all_to_all(
            outgoing.reshape(groups, capacity, PAGE * page_width),
            "grp",
            split_axis=0,
            concat_axis=0,
            tiled=True,
        ),
        lax.all_to_all(
            out_slots.reshape(groups, capacity), "grp", split_axis=0, concat_axis=0, tiled=True
        ),
    )
    chooser = in_slots.reshape(-1)[None, :] == page_ids[:, None]
    stored = jnp.dot(
        chooser.astype(jnp.bfloat16),
        incoming.reshape(groups * capacity, PAGE * page_width),
        preferred_element_type=jnp.float32,
    ).astype(jnp.bfloat16)
    return (
        long_out[None].astype(jnp.bfloat16),
        short_prompt_output[None].astype(jnp.bfloat16),
        stored.reshape(1, page_count, PAGE, page_width),
    )


def solution(mesh):
    in_specs = (
        P("grp", "cp", None),
        P("grp", "cp", None),
        P("grp", "cp", None),
        P("grp", None),
        P("grp", "cp", None),
        P("grp", "cp", None),
        P("grp", "cp", None),
        P("grp", "cp", None),
        P("grp", "cp"),
        P("grp", "cp"),
    )
    out_specs = (P("grp", "cp", None), P("grp", "cp", None), P("grp", "cp", None, None))
    return jax.shard_map(
        per_device, mesh=mesh, in_specs=in_specs, out_specs=out_specs, check_vma=False
    )
```

profile of v0, /device:TPU:1, one launch (start us, length us, event | category | flops | bytes accessed | tf_op | source)
XLA Modules:
  0.0 560.2 jit_solution(17324992464225538733)
XLA Ops:
  3.6 10.0 %all-to-all-start = ((s32[8,1,1]{2,1,0:T(1,128)}), s32[8,1,1]{2,1,0:T(1,128)S(1)}, u32[]{:S(2)}, u32[]{:S(2)}) async-start(s32[8,1,1]{2,1,0:T(1,128)} %copy.214), calls=%async_computation | async-start | bytes 8192 | tf_op jit(solution)/shard_map/all_to_all | solution.py:238
  52.8 7.2 %all-to-all-start.1 = ((bf16[8,2,65536]{2,1,0:T(2,128)(2,1)}), bf16[8,2,65536]{2,1,0:T(2,128)(2,1)}, u32[]{:S(2)}, u32[]{:S(2)}) async-start(bf16[8,2,65536]{2,1,0:T(2,128)(2,1)} %reshape.395), calls=%async_computation.1 | async-start | bytes 4194304 | tf_op jit(solution)/shard_map/all_to_all | solution.py:231
  63.1 476.5 %while.33 = (s32[]{:T(128)}, f32[4,2,256]{2,1,0:T(2,128)}, f32[4,2,256]{2,1,0:T(2,128)S(1)}, f32[4,2,256,128]{3,2,1,0:T(8,128)S(1)}, f32[4,2,256]{2,1,0:T(2,128)...) while((s32[]{:T(128)}, f32[4,2,256]{2,1,0:T(2,128)}, ...), condition=%wide.region_11.12_spmd.clone.clone, body=%wide.region_2.11_spmd.clone.clone.sunk | while | flops 1116625408 | bytes 103596544 | solution.py:183
  76.0 5.6 %collective-permute-done.1 = bf16[256,512]{0,1:T(8,128)(2,1)} collective-permute-done((bf16[256,512]{0,1:T(8,128)(2,1)}, bf16[256,512]{0,1:T(8,128)(2,1)}, u32[]{:S(2)}, u32[]{:S(2)}) %collective-permute-start.1) | collective-permute-done | bytes 262176 | tf_op jit(solution)/shard_map/while/body/eval_jaxpr/ppermute | solution.py:18
  84.5 5.5 collective-permute-done.3
  90.0 26.7 %conditional.9 = ((f32[4,2,256]{2,1,0:T(2,128)}, f32[4,2,256]{2,1,0:T(2,128)S(1)}, f32[4,2,256,128]{3,2,1,0:T(8,128)S(1)}, f32[4,2,256]{2,1,0:T(2,128)}, f32[4,2...) conditional(s32[]{:T(128)} %convert_element_type.89, (f32[4,2,256]{2,1,0:T(2,128)}, f32[4,2,256]{2,1,0:T(2,128)S(1)}, ...), branch_computations={%region_7.7_spmd, %region_8.10_spmd} | conditional | flops 558443520 | bytes 48912780 | solution.py:171
  123.0 20.9 %collective-permute-start = (bf16[256,512]{0,1:T(8,128)(2,1)}, bf16[256,512]{0,1:T(8,128)(2,1)S(1)}, u32[]{:S(2)}, u32[]{:S(2)}) collective-permute-start(bf16[256,512]{0,1:T(8,128)(2,1)} %get-tuple-element.909), channel_id=1, source_target_pairs={{0,8},{1,9},{2,10},{3,11},{4,12},{5,13},{6,14},{7,15},{8,16},{9,17... | collective-permute-start | bytes 786440 | tf_op jit(solution)/shard_map/while/body/eval_jaxpr/ppermute | solution.py:18
  148.7 5.6 %collective-permute-done.1 = bf16[256,512]{0,1:T(8,128)(2,1)} collective-permute-done((bf16[256,512]{0,1:T(8,128)(2,1)}, bf16[256,512]{0,1:T(8,128)(2,1)}, u32[]{:S(2)}, u32[]{:S(2)}) %collective-permute-start.1) | collective-permute-done | bytes 262176 | tf_op jit(solution)/shard_map/while/body/eval_jaxpr/ppermute | solution.py:18
  162.8 26.7 %conditional.9 = ((f32[4,2,256]{2,1,0:T(2,128)}, f32[4,2,256]{2,1,0:T(2,128)S(1)}, f32[4,2,256,128]{3,2,1,0:T(8,128)S(1)}, f32[4,2,256]{2,1,0:T(2,128)}, f32[4,2...) conditional(s32[]{:T(128)} %convert_element_type.89, (f32[4,2,256]{2,1,0:T(2,128)}, f32[4,2,256]{2,1,0:T(2,128)S(1)}, ...), branch_computations={%region_7.7_spmd, %region_8.10_spmd} | conditional | flops 558443520 | bytes 48912780 | solution.py:171
  195.8 29.3 %collective-permute-start = (bf16[256,512]{0,1:T(8,128)(2,1)}, bf16[256,512]{0,1:T(8,128)(2,1)S(1)}, u32[]{:S(2)}, u32[]{:S(2)}) collective-permute-start(bf16[256,512]{0,1:T(8,128)(2,1)} %get-tuple-element.909), channel_id=1, source_target_pairs={{0,8},{1,9},{2,10},{3,11},{4,12},{5,13},{6,14},{7,15},{8,16},{9,17... | collective-permute-start | bytes 786440 | tf_op jit(solution)/shard_map/while/body/eval_jaxpr/ppermute | solution.py:18
  225.1 27.9 %collective-permute-start.1 = (bf16[256,512]{0,1:T(8,128)(2,1)}, bf16[256,512]{0,1:T(8,128)(2,1)}, u32[]{:S(2)}, u32[]{:S(2)}) collective-permute-start(bf16[256,512]{0,1:T(8,128)(2,1)} %get-tuple-element.910), channel_id=1, source_target_pairs={{0,8},{1,9},{2,10},{3,11},{4,12},{5,13},{6,14},{7,15},{8,16},{9,17... | collective-permute-start | bytes 786440 | tf_op jit(solution)/shard_map/while/body/eval_jaxpr/ppermute | solution.py:18
  259.2 26.7 %conditional.9 = ((f32[4,2,256]{2,1,0:T(2,128)}, f32[4,2,256]{2,1,0:T(2,128)S(1)}, f32[4,2,256,128]{3,2,1,0:T(8,128)S(1)}, f32[4,2,256]{2,1,0:T(2,128)}, f32[4,2...) conditional(s32[]{:T(128)} %convert_element_type.89, (f32[4,2,256]{2,1,0:T(2,128)}, f32[4,2,256]{2,1,0:T(2,128)S(1)}, ...), branch_computations={%region_7.7_spmd, %region_8.10_spmd} | conditional | flops 558443520 | bytes 48912780 | solution.py:171
  292.2 12.6 %collective-permute-start = (bf16[256,512]{0,1:T(8,128)(2,1)}, bf16[256,512]{0,1:T(8,128)(2,1)S(1)}, u32[]{:S(2)}, u32[]{:S(2)}) collective-permute-start(bf16[256,512]{0,1:T(8,128)(2,1)} %get-tuple-element.909), channel_id=1, source_target_pairs={{0,8},{1,9},{2,10},{3,11},{4,12},{5,13},{6,14},{7,15},{8,16},{9,17... | collective-permute-start | bytes 786440 | tf_op jit(solution)/shard_map/while/body/eval_jaxpr/ppermute | solution.py:18
  304.9 6.9 %collective-permute-start.1 = (bf16[256,512]{0,1:T(8,128)(2,1)}, bf16[256,512]{0,1:T(8,128)(2,1)}, u32[]{:S(2)}, u32[]{:S(2)}) collective-permute-start(bf16[256,512]{0,1:T(8,128)(2,1)} %get-tuple-element.910), channel_id=1, source_target_pairs={{0,8},{1,9},{2,10},{3,11},{4,12},{5,13},{6,14},{7,15},{8,16},{9,17... | collective-permute-start | bytes 786440 | tf_op jit(solution)/shard_map/while/body/eval_jaxpr/ppermute | solution.py:18
  322.6 26.7 %conditional.9 = ((f32[4,2,256]{2,1,0:T(2,128)}, f32[4,2,256]{2,1,0:T(2,128)S(1)}, f32[4,2,256,128]{3,2,1,0:T(8,128)S(1)}, f32[4,2,256]{2,1,0:T(2,128)}, f32[4,2...) conditional(s32[]{:T(128)} %convert_element_type.89, (f32[4,2,256]{2,1,0:T(2,128)}, f32[4,2,256]{2,1,0:T(2,128)S(1)}, ...), branch_computations={%region_7.7_spmd, %region_8.10_spmd} | conditional | flops 558443520 | bytes 48912780 | solution.py:171
  355.6 18.0 %collective-permute-start = (bf16[256,512]{0,1:T(8,128)(2,1)}, bf16[256,512]{0,1:T(8,128)(2,1)S(1)}, u32[]{:S(2)}, u32[]{:S(2)}) collective-permute-start(bf16[256,512]{0,1:T(8,128)(2,1)} %get-tuple-element.909), channel_id=1, source_target_pairs={{0,8},{1,9},{2,10},{3,11},{4,12},{5,13},{6,14},{7,15},{8,16},{9,17... | collective-permute-start | bytes 786440 | tf_op jit(solution)/shard_map/while/body/eval_jaxpr/ppermute | solution.py:18
  373.6 11.9 %collective-permute-start.1 = (bf16[256,512]{0,1:T(8,128)(2,1)}, bf16[256,512]{0,1:T(8,128)(2,1)}, u32[]{:S(2)}, u32[]{:S(2)}) collective-permute-start(bf16[256,512]{0,1:T(8,128)(2,1)} %get-tuple-element.910), channel_id=1, source_target_pairs={{0,8},{1,9},{2,10},{3,11},{4,12},{5,13},{6,14},{7,15},{8,16},{9,17... | collective-permute-start | bytes 786440 | tf_op jit(solution)/shard_map/while/body/eval_jaxpr/ppermute | solution.py:18
  391.3 26.7 %conditional.9 = ((f32[4,2,256]{2,1,0:T(2,128)}, f32[4,2,256]{2,1,0:T(2,128)S(1)}, f32[4,2,256,128]{3,2,1,0:T(8,128)S(1)}, f32[4,2,256]{2,1,0:T(2,128)}, f32[4,2...) conditional(s32[]{:T(128)} %convert_element_type.89, (f32[4,2,256]{2,1,0:T(2,128)}, f32[4,2,256]{2,1,0:T(2,128)S(1)}, ...), branch_computations={%region_7.7_spmd, %region_8.10_spmd} | conditional | flops 558443520 | bytes 48912780 | solution.py:171
  424.3 11.8 %collective-permute-start = (bf16[256,512]{0,1:T(8,128)(2,1)}, bf16[256,512]{0,1:T(8,128)(2,1)S(1)}, u32[]{:S(2)}, u32[]{:S(2)}) collective-permute-start(bf16[256,512]{0,1:T(8,128)(2,1)} %get-tuple-element.909), channel_id=1, source_target_pairs={{0,8},{1,9},{2,10},{3,11},{4,12},{5,13},{6,14},{7,15},{8,16},{9,17... | collective-permute-start | bytes 786440 | tf_op jit(solution)/shard_map/while/body/eval_jaxpr/ppermute | solution.py:18
  436.1 6.9 %collective-permute-start.1 = (bf16[256,512]{0,1:T(8,128)(2,1)}, bf16[256,512]{0,1:T(8,128)(2,1)}, u32[]{:S(2)}, u32[]{:S(2)}) collective-permute-start(bf16[256,512]{0,1:T(8,128)(2,1)} %get-tuple-element.910), channel_id=1, source_target_pairs={{0,8},{1,9},{2,10},{3,11},{4,12},{5,13},{6,14},{7,15},{8,16},{9,17... | collective-permute-start | bytes 786440 | tf_op jit(solution)/shard_map/while/body/eval_jaxpr/ppermute | solution.py:18
  452.7 26.7 %conditional.9 = ((f32[4,2,256]{2,1,0:T(2,128)}, f32[4,2,256]{2,1,0:T(2,128)S(1)}, f32[4,2,256,128]{3,2,1,0:T(8,128)S(1)}, f32[4,2,256]{2,1,0:T(2,128)}, f32[4,2...) conditional(s32[]{:T(128)} %convert_element_type.89, (f32[4,2,256]{2,1,0:T(2,128)}, f32[4,2,256]{2,1,0:T(2,128)S(1)}, ...), branch_computations={%region_7.7_spmd, %region_8.10_spmd} | conditional | flops 558443520 | bytes 48912780 | solution.py:171
  485.7 7.5 %collective-permute-start = (bf16[256,512]{0,1:T(8,128)(2,1)}, bf16[256,512]{0,1:T(8,128)(2,1)S(1)}, u32[]{:S(2)}, u32[]{:S(2)}) collective-permute-start(bf16[256,512]{0,1:T(8,128)(2,1)} %get-tuple-element.909), channel_id=1, source_target_pairs={{0,8},{1,9},{2,10},{3,11},{4,12},{5,13},{6,14},{7,15},{8,16},{9,17... | collective-permute-start | bytes 786440 | tf_op jit(solution)/shard_map/while/body/eval_jaxpr/ppermute | solution.py:18
  509.2 26.7 %conditional.9 = ((f32[4,2,256]{2,1,0:T(2,128)}, f32[4,2,256]{2,1,0:T(2,128)S(1)}, f32[4,2,256,128]{3,2,1,0:T(8,128)S(1)}, f32[4,2,256]{2,1,0:T(2,128)}, f32[4,2...) conditional(s32[]{:T(128)} %convert_element_type.89, (f32[4,2,256]{2,1,0:T(2,128)}, f32[4,2,256]{2,1,0:T(2,128)S(1)}, ...), branch_computations={%region_7.7_spmd, %region_8.10_spmd} | conditional | flops 558443520 | bytes 48912780 | solution.py:171
  547.5 6.7 %reshape.396 = bf16[8,1,131072]{2,1,0:T(2,128)(2,1)} reshape(bf16[8,2,65536]{2,1,0:T(2,128)(2,1)} %all-to-all-done.1) | data formatting | bytes 4194304
  (454 shorter events, 363.2 us)
Async XLA Ops:
  3.6 49.1 %all-to-all-start = ((s32[8,1,1]{2,1,0:T(1,128)}), s32[8,1,1]{2,1,0:T(1,128)S(1)}, u32[]{:S(2)}, u32[]{:S(2)}) async-start(s32[8,1,1]{2,1,0:T(1,128)} %copy.214), calls=%async_computation | async-start | bytes 8192 | tf_op jit(solution)/shard_map/all_to_all | solution.py:238
  52.8 494.7 %all-to-all-start.1 = ((bf16[8,2,65536]{2,1,0:T(2,128)(2,1)}), bf16[8,2,65536]{2,1,0:T(2,128)(2,1)}, u32[]{:S(2)}, u32[]{:S(2)}) async-start(bf16[8,2,65536]{2,1,0:T(2,128)(2,1)} %reshape.395), calls=%async_computation.1 | async-start | bytes 4194304 | tf_op jit(solution)/shard_map/all_to_all | solution.py:231
  63.1 21.4 %collective-permute-start.2 = (bf16[512,512]{0,1:T(8,128)(2,1)}, bf16[512,512]{0,1:T(8,128)(2,1)}, u32[]{:S(2)}, u32[]{:S(2)}) collective-permute-start(bf16[512,512]{0,1:T(8,128)(2,1)} %get-tuple-element.911), channel_id=1, source_target_pairs={{8,0},{9,1},{10,2},{11,3},{12,4},{13,5},{14,6},{15,7},{16,8},{17,9... | collective-permute-start | bytes 1572872 | tf_op jit(solution)/shard_map/while/body/eval_jaxpr/ppermute | solution.py:18
  64.4 25.6 %collective-permute-start.3 = (bf16[512,512]{0,1:T(8,128)(2,1)}, bf16[512,512]{0,1:T(8,128)(2,1)}, u32[]{:S(2)}, u32[]{:S(2)}) collective-permute-start(bf16[512,512]{0,1:T(8,128)(2,1)} %get-tuple-element.912), channel_id=1, source_target_pairs={{8,0},{9,1},{10,2},{11,3},{12,4},{13,5},{14,6},{15,7},{16,8},{17,9... | collective-permute-start | bytes 1572872 | tf_op jit(solution)/shard_map/while/body/eval_jaxpr/ppermute | solution.py:18
  120.5 36.8 %collective-permute-start.2 = (bf16[512,512]{0,1:T(8,128)(2,1)}, bf16[512,512]{0,1:T(8,128)(2,1)}, u32[]{:S(2)}, u32[]{:S(2)}) collective-permute-start(bf16[512,512]{0,1:T(8,128)(2,1)} %get-tuple-element.911), channel_id=1, source_target_pairs={{8,0},{9,1},{10,2},{11,3},{12,4},{13,5},{14,6},{15,7},{16,8},{17,9... | collective-permute-start | bytes 1572872 | tf_op jit(solution)/shard_map/while/body/eval_jaxpr/ppermute | solution.py:18
  121.7 41.0 %collective-permute-start.3 = (bf16[512,512]{0,1:T(8,128)(2,1)}, bf16[512,512]{0,1:T(8,128)(2,1)}, u32[]{:S(2)}, u32[]{:S(2)}) collective-permute-start(bf16[512,512]{0,1:T(8,128)(2,1)} %get-tuple-element.912), channel_id=1, source_target_pairs={{8,0},{9,1},{10,2},{11,3},{12,4},{13,5},{14,6},{15,7},{16,8},{17,9... | collective-permute-start | bytes 1572872 | tf_op jit(solution)/shard_map/while/body/eval_jaxpr/ppermute | solution.py:18
  123.0 25.7 %collective-permute-start = (bf16[256,512]{0,1:T(8,128)(2,1)}, bf16[256,512]{0,1:T(8,128)(2,1)S(1)}, u32[]{:S(2)}, u32[]{:S(2)}) collective-permute-start(bf16[256,512]{0,1:T(8,128)(2,1)} %get-tuple-element.909), channel_id=1, source_target_pairs={{0,8},{1,9},{2,10},{3,11},{4,12},{5,13},{6,14},{7,15},{8,16},{9,17... | collective-permute-start | bytes 786440 | tf_op jit(solution)/shard_map/while/body/eval_jaxpr/ppermute | solution.py:18
  193.2 66.0 %collective-permute-start.2 = (bf16[512,512]{0,1:T(8,128)(2,1)}, bf16[512,512]{0,1:T(8,128)(2,1)}, u32[]{:S(2)}, u32[]{:S(2)}) collective-permute-start(bf16[512,512]{0,1:T(8,128)(2,1)} %get-tuple-element.911), channel_id=1, source_target_pairs={{8,0},{9,1},{10,2},{11,3},{12,4},{13,5},{14,6},{15,7},{16,8},{17,9... | collective-permute-start | bytes 1572872 | tf_op jit(solution)/shard_map/while/body/eval_jaxpr/ppermute | solution.py:18
  194.5 64.7 %collective-permute-start.3 = (bf16[512,512]{0,1:T(8,128)(2,1)}, bf16[512,512]{0,1:T(8,128)(2,1)}, u32[]{:S(2)}, u32[]{:S(2)}) collective-permute-start(bf16[512,512]{0,1:T(8,128)(2,1)} %get-tuple-element.912), channel_id=1, source_target_pairs={{8,0},{9,1},{10,2},{11,3},{12,4},{13,5},{14,6},{15,7},{16,8},{17,9... | collective-permute-start | bytes 1572872 | tf_op jit(solution)/shard_map/while/body/eval_jaxpr/ppermute | solution.py:18
  195.8 57.8 %collective-permute-start = (bf16[256,512]{0,1:T(8,128)(2,1)}, bf16[256,512]{0,1:T(8,128)(2,1)S(1)}, u32[]{:S(2)}, u32[]{:S(2)}) collective-permute-start(bf16[256,512]{0,1:T(8,128)(2,1)} %get-tuple-element.909), channel_id=1, source_target_pairs={{0,8},{1,9},{2,10},{3,11},{4,12},{5,13},{6,14},{7,15},{8,16},{9,17... | collective-permute-start | bytes 786440 | tf_op jit(solution)/shard_map/while/body/eval_jaxpr/ppermute | solution.py:18
  225.1 31.2 %collective-permute-start.1 = (bf16[256,512]{0,1:T(8,128)(2,1)}, bf16[256,512]{0,1:T(8,128)(2,1)}, u32[]{:S(2)}, u32[]{:S(2)}) collective-permute-start(bf16[256,512]{0,1:T(8,128)(2,1)} %get-tuple-element.910), channel_id=1, source_target_pairs={{0,8},{1,9},{2,10},{3,11},{4,12},{5,13},{6,14},{7,15},{8,16},{9,17... | collective-permute-start | bytes 786440 | tf_op jit(solution)/shard_map/while/body/eval_jaxpr/ppermute | solution.py:18
  289.6 27.9 %collective-permute-start.2 = (bf16[512,512]{0,1:T(8,128)(2,1)}, bf16[512,512]{0,1:T(8,128)(2,1)}, u32[]{:S(2)}, u32[]{:S(2)}) collective-permute-start(bf16[512,512]{0,1:T(8,128)(2,1)} %get-tuple-element.911), channel_id=1, source_target_pairs={{8,0},{9,1},{10,2},{11,3},{12,4},{13,5},{14,6},{15,7},{16,8},{17,9... | collective-permute-start | bytes 1572872 | tf_op jit(solution)/shard_map/while/body/eval_jaxpr/ppermute | solution.py:18
  290.9 31.6 %collective-permute-start.3 = (bf16[512,512]{0,1:T(8,128)(2,1)}, bf16[512,512]{0,1:T(8,128)(2,1)}, u32[]{:S(2)}, u32[]{:S(2)}) collective-permute-start(bf16[512,512]{0,1:T(8,128)(2,1)} %get-tuple-element.912), channel_id=1, source_target_pairs={{8,0},{9,1},{10,2},{11,3},{12,4},{13,5},{14,6},{15,7},{16,8},{17,9... | collective-permute-start | bytes 1572872 | tf_op jit(solution)/shard_map/while/body/eval_jaxpr/ppermute | solution.py:18
  292.2 20.1 %collective-permute-start = (bf16[256,512]{0,1:T(8,128)(2,1)}, bf16[256,512]{0,1:T(8,128)(2,1)S(1)}, u32[]{:S(2)}, u32[]{:S(2)}) collective-permute-start(bf16[256,512]{0,1:T(8,128)(2,1)} %get-tuple-element.909), channel_id=1, source_target_pairs={{0,8},{1,9},{2,10},{3,11},{4,12},{5,13},{6,14},{7,15},{8,16},{9,17... | collective-permute-start | bytes 786440 | tf_op jit(solution)/shard_map/while/body/eval_jaxpr/ppermute | solution.py:18
  353.0 38.3 %collective-permute-start.2 = (bf16[512,512]{0,1:T(8,128)(2,1)}, bf16[512,512]{0,1:T(8,128)(2,1)}, u32[]{:S(2)}, u32[]{:S(2)}) collective-permute-start(bf16[512,512]{0,1:T(8,128)(2,1)} %get-tuple-element.911), channel_id=1, source_target_pairs={{8,0},{9,1},{10,2},{11,3},{12,4},{13,5},{14,6},{15,7},{16,8},{17,9... | collective-permute-start | bytes 1572872 | tf_op jit(solution)/shard_map/while/body/eval_jaxpr/ppermute | solution.py:18
  354.3 37.0 %collective-permute-start.3 = (bf16[512,512]{0,1:T(8,128)(2,1)}, bf16[512,512]{0,1:T(8,128)(2,1)}, u32[]{:S(2)}, u32[]{:S(2)}) collective-permute-start(bf16[512,512]{0,1:T(8,128)(2,1)} %get-tuple-element.912), channel_id=1, source_target_pairs={{8,0},{9,1},{10,2},{11,3},{12,4},{13,5},{14,6},{15,7},{16,8},{17,9... | collective-permute-start | bytes 1572872 | tf_op jit(solution)/shard_map/while/body/eval_jaxpr/ppermute | solution.py:18
  355.6 30.4 %collective-permute-start = (bf16[256,512]{0,1:T(8,128)(2,1)}, bf16[256,512]{0,1:T(8,128)(2,1)S(1)}, u32[]{:S(2)}, u32[]{:S(2)}) collective-permute-start(bf16[256,512]{0,1:T(8,128)(2,1)} %get-tuple-element.909), channel_id=1, source_target_pairs={{0,8},{1,9},{2,10},{3,11},{4,12},{5,13},{6,14},{7,15},{8,16},{9,17... | collective-permute-start | bytes 786440 | tf_op jit(solution)/shard_map/while/body/eval_jaxpr/ppermute | solution.py:18
  373.6 14.7 %collective-permute-start.1 = (bf16[256,512]{0,1:T(8,128)(2,1)}, bf16[256,512]{0,1:T(8,128)(2,1)}, u32[]{:S(2)}, u32[]{:S(2)}) collective-permute-start(bf16[256,512]{0,1:T(8,128)(2,1)} %get-tuple-element.910), channel_id=1, source_target_pairs={{0,8},{1,9},{2,10},{3,11},{4,12},{5,13},{6,14},{7,15},{8,16},{9,17... | collective-permute-start | bytes 786440 | tf_op jit(solution)/shard_map/while/body/eval_jaxpr/ppermute | solution.py:18
  421.7 27.7 %collective-permute-start.2 = (bf16[512,512]{0,1:T(8,128)(2,1)}, bf16[512,512]{0,1:T(8,128)(2,1)}, u32[]{:S(2)}, u32[]{:S(2)}) collective-permute-start(bf16[512,512]{0,1:T(8,128)(2,1)} %get-tuple-element.911), channel_id=1, source_target_pairs={{8,0},{9,1},{10,2},{11,3},{12,4},{13,5},{14,6},{15,7},{16,8},{17,9... | collective-permute-start | bytes 1572872 | tf_op jit(solution)/shard_map/while/body/eval_jaxpr/ppermute | solution.py:18
  423.0 29.6 %collective-permute-start.3 = (bf16[512,512]{0,1:T(8,128)(2,1)}, bf16[512,512]{0,1:T(8,128)(2,1)}, u32[]{:S(2)}, u32[]{:S(2)}) collective-permute-start(bf16[512,512]{0,1:T(8,128)(2,1)} %get-tuple-element.912), channel_id=1, source_target_pairs={{8,0},{9,1},{10,2},{11,3},{12,4},{13,5},{14,6},{15,7},{16,8},{17,9... | collective-permute-start | bytes 1572872 | tf_op jit(solution)/shard_map/while/body/eval_jaxpr/ppermute | solution.py:18
  424.3 19.3 %collective-permute-start = (bf16[256,512]{0,1:T(8,128)(2,1)}, bf16[256,512]{0,1:T(8,128)(2,1)S(1)}, u32[]{:S(2)}, u32[]{:S(2)}) collective-permute-start(bf16[256,512]{0,1:T(8,128)(2,1)} %get-tuple-element.909), channel_id=1, source_target_pairs={{0,8},{1,9},{2,10},{3,11},{4,12},{5,13},{6,14},{7,15},{8,16},{9,17... | collective-permute-start | bytes 786440 | tf_op jit(solution)/shard_map/while/body/eval_jaxpr/ppermute | solution.py:18
  483.1 21.7 %collective-permute-start.2 = (bf16[512,512]{0,1:T(8,128)(2,1)}, bf16[512,512]{0,1:T(8,128)(2,1)}, u32[]{:S(2)}, u32[]{:S(2)}) collective-permute-start(bf16[512,512]{0,1:T(8,128)(2,1)} %get-tuple-element.911), channel_id=1, source_target_pairs={{8,0},{9,1},{10,2},{11,3},{12,4},{13,5},{14,6},{15,7},{16,8},{17,9... | collective-permute-start | bytes 1572872 | tf_op jit(solution)/shard_map/while/body/eval_jaxpr/ppermute | solution.py:18
  484.4 24.8 %collective-permute-start.3 = (bf16[512,512]{0,1:T(8,128)(2,1)}, bf16[512,512]{0,1:T(8,128)(2,1)}, u32[]{:S(2)}, u32[]{:S(2)}) collective-permute-start(bf16[512,512]{0,1:T(8,128)(2,1)} %get-tuple-element.912), channel_id=1, source_target_pairs={{8,0},{9,1},{10,2},{11,3},{12,4},{13,5},{14,6},{15,7},{16,8},{17,9... | collective-permute-start | bytes 1572872 | tf_op jit(solution)/shard_map/while/body/eval_jaxpr/ppermute | solution.py:18
  485.7 12.1 %collective-permute-start = (bf16[256,512]{0,1:T(8,128)(2,1)}, bf16[256,512]{0,1:T(8,128)(2,1)S(1)}, u32[]{:S(2)}, u32[]{:S(2)}) collective-permute-start(bf16[256,512]{0,1:T(8,128)(2,1)} %get-tuple-element.909), channel_id=1, source_target_pairs={{0,8},{1,9},{2,10},{3,11},{4,12},{5,13},{6,14},{7,15},{8,16},{9,17... | collective-permute-start | bytes 786440 | tf_op jit(solution)/shard_map/while/body/eval_jaxpr/ppermute | solution.py:18
  (88 other events, 405.0 us)
where the time goes:
time: 567 us; the launch traced here: 560 us
  starting transfers between devices  206 us (36%)
  local copies, waits for them, and re-layouts  154 us (27%)
  other arithmetic  92.2 us (16%)
  matrix products  55.5 us (10%)
  waiting for transfers between devices  50.4 us (9%)
    ppermute x28, starting transfers between devices, shifted(): return lax.ppermute(x, axis, pairs)  189 us
    ppermute x28, waiting for transfers between devices, shifted(): return lax.ppermute(x, axis, pairs)  50.4 us
    while x28, local copies, waits for them, and re-layouts  42.8 us
    dot_general x9, matrix products, block_stats(): jnp.einsum('pgjrk,pkgd->pgjrd', weights.astype(jnp.bfloat16), value_head_...  28.2 us
    select_n x14, other arithmetic, select_stats(): jnp.where(condition, left_leaf, right_leaf)  27.5 us
    another operation x14, local copies, waits for them, and re-layouts, absorb(): keys_pair = jnp.stack([key_lead, jnp.where(below_self, key_lead, key_tail)])  25.2 us
    another operation x14, local copies, waits for them, and re-layouts, absorb(): jnp.stack([jnp.where(below_self, query_first, query_second), query_second])  21.3 us
    dot_general x9, matrix products, head_scores(): jnp.einsum('prgjd,pkgd->pgjrk', grouped_heads, key_head_rows, preferred_e...  18.7 us
  transfers between devices with their start and end apart: 30, of which 14 were waited for; matrix products, arithmetic and copies ran while one was open for 49% of the time, Pallas kernels for 0%

commit v1 on v0

v1 whole, which is shorter than its diff:
```python
import math

import jax
import jax.numpy as jnp
from jax import lax
from jax.experimental import pallas as pl
from jax.experimental.pallas import tpu as pltpu
from jax.sharding import Mesh
from jax.sharding import PartitionSpec as P

QUERY_HEADS = 8
KEY_VALUE_HEADS = 4
HEAD_SIZE = 128
PAGE = 128
SPAN = 8


def head_scores(query_rows, key_row_block, visible):
    paired_count, count_of_rows = (query_rows.shape[0], query_rows.shape[1])
    grouped_heads = query_rows.reshape(
        paired_count, count_of_rows, KEY_VALUE_HEADS, QUERY_HEADS // KEY_VALUE_HEADS, HEAD_SIZE
    )
    key_head_rows = key_row_block.reshape(
        paired_count, key_row_block.shape[1], KEY_VALUE_HEADS, HEAD_SIZE
    )
    scores = jnp.einsum(
        "prgjd,pkgd->pgjrk", grouped_heads, key_head_rows, preferred_element_type=jnp.float32
    )
    scores = scores / math.sqrt(HEAD_SIZE)
    return jnp.where(visible[:, None, None], scores, -jnp.inf)


def block_stats(query_rows, key_row_block, value_row_block, visible):
    scores = head_scores(query_rows, key_row_block, visible)
    highest = jnp.max(scores, axis=-1)
    anchor = jnp.where(jnp.isfinite(highest), highest, 0.0)
    weights = jnp.where(visible[:, None, None], jnp.exp(scores - anchor[..., None]), 0.0)
    weight_sum = jnp.sum(weights, axis=-1)
    value_head_rows = value_row_block.reshape(
        value_row_block.shape[0], value_row_block.shape[1], KEY_VALUE_HEADS, HEAD_SIZE
    )
    summed = jnp.einsum(
        "pgjrk,pkgd->pgjrd",
        weights.astype(jnp.bfloat16),
        value_head_rows,
        preferred_element_type=jnp.float32,
    )
    return (highest, weight_sum, summed)


def take_pair(pair_stats, position_in):
    return jax.tree.map(lambda leaf_array: leaf_array[position_in], pair_stats)


def finish_rows(stats_in, live_rows):
    highest, weight_sum, summed = stats_in
    divisor = jnp.where(weight_sum > 0, weight_sum, 1.0)
    result = summed / divisor[..., None]
    result = jnp.where(live_rows[None, None, :, None], result, 0.0)
    return jnp.transpose(result, (2, 0, 1, 3)).reshape(live_rows.shape[0], QUERY_HEADS * HEAD_SIZE)


def flash_kernel(info_ref, q_ref, k_ref, v_ref, o_ref, m_sc, l_sc, acc_sc, *, block, blocks):
    qb = pl.program_id(0)
    kc = pl.program_id(1)
    member = info_ref[0]
    length = info_ref[1]
    bq = jnp.where(qb == 0, member, 2 * SPAN - 1 - member)
    kmax = jnp.minimum(bq, (length - 1) // block)

    @pl.when(kc == 0)
    def _init():
        m_sc[...] = jnp.full(m_sc.shape, -jnp.inf, jnp.float32)
        l_sc[...] = jnp.zeros(l_sc.shape, jnp.float32)
        acc_sc[...] = jnp.zeros(acc_sc.shape, jnp.float32)

    @pl.when(kc <= kmax)
    def _step():
        q_pos = bq * block + lax.broadcasted_iota(jnp.int32, (block, block), 0)
        k_pos = kc * block + lax.broadcasted_iota(jnp.int32, (block, block), 1)
        visible = (k_pos <= q_pos) & (k_pos < length) & (q_pos < length)
        scale = 1.0 / math.sqrt(HEAD_SIZE)
        for g in range(KEY_VALUE_HEADS):
            k = k_ref[0, :, g * HEAD_SIZE:(g + 1) * HEAD_SIZE]
            v = v_ref[0, :, g * HEAD_SIZE:(g + 1) * HEAD_SIZE]
            for jj in range(QUERY_HEADS // KEY_VALUE_HEADS):
                h = g * (QUERY_HEADS // KEY_VALUE_HEADS) + jj
                q = q_ref[:, h * HEAD_SIZE:(h + 1) * HEAD_SIZE]
                s = lax.dot_general(
                    q, k, (((1,), (1,)), ((), ())), preferred_element_type=jnp.float32
                ) * scale
                s = jnp.where(visible, s, -jnp.inf)
                m_old = m_sc[h]
                m_new = jnp.maximum(m_old, jnp.max(s, axis=-1, keepdims=True))
                anchor = jnp.where(m_new > -jnp.inf, m_new, 0.0)
                p = jnp.where(visible, jnp.exp(s - anchor), 0.0)
                alpha = jnp.exp(m_old - anchor)
                l_sc[h] = alpha * l_sc[h] + jnp.sum(p, axis=-1, keepdims=True)
                acc_sc[h] = alpha * acc_sc[h] + jnp.dot(
                    p.astype(jnp.bfloat16), v, preferred_element_type=jnp.float32
                )
                m_sc[h] = m_new

    @pl.when(kc == blocks - 1)
    def _finish():
        for h in range(QUERY_HEADS):
            l = l_sc[h]
            divisor = jnp.where(l > 0, l, 1.0)
            o_ref[:, h * HEAD_SIZE:(h + 1) * HEAD_SIZE] = (acc_sc[h] / divisor).astype(o_ref.dtype)


def long_attention(info, query_rows, kv_all, block):
    blocks = 2 * SPAN
    half_kv = kv_all.shape[-1] // 2

    def kv_index(qb, kc, info_ref, which):
        member = info_ref[0]
        length = info_ref[1]
        bq = jnp.where(qb == 0, member, 2 * SPAN - 1 - member)
        kk = jnp.minimum(kc, jnp.minimum(bq, (length - 1) // block))
        j = jnp.where(kk < SPAN, 2 * kk, 2 * (2 * SPAN - 1 - kk) + 1)
        return (j, 0, which)

    grid_spec = pltpu.PrefetchScalarGridSpec(
        num_scalar_prefetch=1,
        grid=(2, blocks),
        in_specs=[
            pl.BlockSpec((block, query_rows.shape[1]), lambda qb, kc, info_ref: (qb, 0)),
            pl.BlockSpec((1, block, half_kv), lambda qb, kc, info_ref: kv_index(qb, kc, info_ref, 0)),
            pl.BlockSpec((1, block, half_kv), lambda qb, kc, info_ref: kv_index(qb, kc, info_ref, 1)),
        ],
        out_specs=pl.BlockSpec((block, query_rows.shape[1]), lambda qb, kc, info_ref: (qb, 0)),
        scratch_shapes=[
            pltpu.VMEM((QUERY_HEADS, block, 1), jnp.float32),
            pltpu.VMEM((QUERY_HEADS, block, 1), jnp.float32),
            pltpu.VMEM((QUERY_HEADS, block, HEAD_SIZE), jnp.float32),
        ],
    )
    flops = 4 * 17 * block * block * HEAD_SIZE * QUERY_HEADS
    return pl.pallas_call(
        lambda *refs: flash_kernel(*refs, block=block, blocks=blocks),
        grid_spec=grid_spec,
        out_shape=jax.ShapeDtypeStruct(query_rows.shape, jnp.bfloat16),
        compiler_params=pltpu.CompilerParams(
            dimension_semantics=("arbitrary", "arbitrary"),
        ),
        cost_estimate=pl.CostEstimate(
            flops=flops,
            transcendentals=17 * block * block * QUERY_HEADS,
            bytes_accessed=2 * query_rows.size * 2 + 17 * block * kv_all.shape[-1] * 2,
        ),
        name="long_flash",
    )(info, query_rows, kv_all, kv_all)


def per_device(
    query_long,
    long_prompt_keys,
    long_prompt_values,
    long_length,
    short_prompt_queries,
    short_prompt_keys,
    short_prompt_values,
    short_prompt_index,
    page_owner,
    page_slot,
):
    half_rows = query_long.shape[1] // 2
    member = lax.axis_index("m")
    group_id = lax.axis_index("r")
    length = lax.dynamic_index_in_dim(long_length[0], group_id, 0, keepdims=False)
    offsets = jnp.arange(half_rows, dtype=jnp.int32)
    pos_first = member * half_rows + offsets
    pos_second = (2 * SPAN - 1 - member) * half_rows + offsets

    key_row_block = long_prompt_keys[0]
    value_row_block = long_prompt_values[0]
    kv_rows = jnp.concatenate([key_row_block, value_row_block], axis=-1)

    kv_all = lax.all_gather(kv_rows, "m", axis=0, tiled=False)
    kv_all = kv_all.reshape(2 * SPAN, half_rows, kv_rows.shape[-1])
    info = jnp.stack([member, length]).astype(jnp.int32)
    long_out = long_attention(info, query_long[0], kv_all, half_rows)

    segment_row = short_prompt_index[0, 0]
    order_ids = jnp.arange(segment_row.shape[0], dtype=jnp.int32)
    short_visible = (order_ids[None, :] <= order_ids[:, None]) & (
        segment_row[None, :] == segment_row[:, None]
    )
    short_stats = block_stats(
        short_prompt_queries[0][None],
        short_prompt_keys[0][None],
        short_prompt_values[0][None],
        short_visible[None],
    )
    short_prompt_output = finish_rows(take_pair(short_stats, 0), order_ids >= 0)

    row_positions = jnp.concatenate([pos_first, pos_second])
    kv_rows = jnp.where((row_positions < length)[:, None], kv_rows, jnp.zeros_like(kv_rows))
    page_count = kv_rows.shape[0] // PAGE
    page_width = kv_rows.shape[1]
    page_data = kv_rows.reshape(page_count, PAGE * page_width)
    owners = page_owner[0]
    slot_ids = page_slot[0]
    groups = lax.axis_size("grp")
    capacity = max(1, page_count // groups)
    page_ids = jnp.arange(page_count, dtype=jnp.int32)
    earlier = jnp.sum(
        (owners[None, :] == owners[:, None]) & (page_ids[None, :] < page_ids[:, None]), axis=1
    )
    target = owners * capacity + earlier
    bucket_ids = jnp.arange(groups * capacity, dtype=jnp.int32)
    onehot = target[None, :] == bucket_ids[:, None]
    outgoing = jnp.dot(
        onehot.astype(jnp.bfloat16), page_data, preferred_element_type=jnp.float32
    ).astype(jnp.bfloat16)
    out_slots = jnp.max(jnp.where(onehot, slot_ids[None, :], -1), axis=1)
    incoming, in_slots = (
        lax.all_to_all(
            outgoing.reshape(groups, capacity, PAGE * page_width),
            "grp",
            split_axis=0,
            concat_axis=0,
            tiled=True,
        ),
        lax.all_to_all(
            out_slots.reshape(groups, capacity), "grp", split_axis=0, concat_axis=0, tiled=True
        ),
    )
    chooser = in_slots.reshape(-1)[None, :] == page_ids[:, None]
    stored = jnp.dot(
        chooser.astype(jnp.bfloat16),
        incoming.reshape(groups * capacity, PAGE * page_width),
        preferred_element_type=jnp.float32,
    ).astype(jnp.bfloat16)
    return (
        long_out[None],
        short_prompt_output[None].astype(jnp.bfloat16),
        stored.reshape(1, page_count, PAGE, page_width),
    )


def solution(mesh):
    n_grp = mesh.shape["grp"]
    n_cp = mesh.shape["cp"]
    stride = n_cp // SPAN
    split_mesh = Mesh(mesh.devices.reshape(n_grp, SPAN, stride), ("grp", "m", "r"))
    rows = ("m", "r")
    in_specs = (
        P("grp", rows, None),
        P("grp", rows, None),
        P("grp", rows, None),
        P("grp", None),
        P("grp", rows, None),
        P("grp", rows, None),
        P("grp", rows, None),
        P("grp", rows, None),
        P("grp", rows),
        P("grp", rows),
    )
    out_specs = (P("grp", rows, None), P("grp", rows, None), P("grp", rows, None, None))
    return jax.shard_map(
        per_device, mesh=split_mesh, in_specs=in_specs, out_specs=out_specs, check_vma=False
    )
```

time: 567 us -> 239 us (0.42)
  starting transfers between devices: 206 us -> 17.5 us
  local copies, waits for them, and re-layouts: 154 us -> 14.8 us
  other arithmetic: 92.2 us -> 8.7 us
  Pallas kernels: 0 us -> 71 us
  waiting for transfers between devices: 50.4 us -> 102 us
  matrix products: 55.5 us -> 7.63 us
  between operations: 0.99 us -> 14.2 us
    ppermute x28 -> x0, starting transfers between devices: 189 us -> none  [shifted(): return lax.ppermute(x, axis, pairs)]
    pallas_call x0 -> x1, Pallas kernels: none -> 71 us  [long_attention(): pl.pallas_call(lambda *refs: flash_kernel(*refs, block=block, blocks=bloc...]
    all_to_all x1, waiting for transfers between devices: 0.01 us -> 68.6 us  [per_device(): lax.all_to_all(outgoing.reshape(groups, capacity, PAGE * page_width), 'gr...]
    another operation x49 -> x3, local copies, waits for them, and re-layouts: 66 us -> 0.32 us  [the longest x14 25.2 us: absorb(): keys_pair = jnp.stack([key_lead, jnp.where(below_self, key_lead, key_tail)])]
    ppermute x28 -> x0, waiting for transfers between devices: 50.4 us -> none  [shifted(): return lax.ppermute(x, axis, pairs)]
    while x28 -> x0, local copies, waits for them, and re-layouts: 42.8 us -> none
    select_n x28 -> x0, other arithmetic: 38.3 us -> none  [the longest x14 27.5 us: select_stats(): jnp.where(condition, left_leaf, right_leaf)]
    all_gather x0 -> x1, waiting for transfers between devices: none -> 33.6 us  [per_device(): kv_all = lax.all_gather(kv_rows, 'm', axis=0, tiled=False)]
  transfers between devices with their start and end apart: 30 -> 3, of which waited for: 14 -> 2; matrix products, arithmetic and copies ran while one was open for 49% -> 12% of each run, Pallas kernels for 0% -> 0%
where the time goes in v1:
time: 239 us; the launch traced here: 236 us
  waiting for transfers between devices  102 us (43%)
  Pallas kernels  71 us (30%)
  starting transfers between devices  17.5 us (7%)
  local copies, waits for them, and re-layouts  14.8 us (6%)
  between operations  14.2 us (6%)
  other arithmetic  8.7 us (4%)
  matrix products  7.63 us (3%)
    pallas_call x1, Pallas kernels, long_attention(): pl.pallas_call(lambda *refs: flash_kernel(*refs, block=block, blocks=bloc...  71 us
    all_to_all x1, waiting for transfers between devices, per_device(): lax.all_to_all(outgoing.reshape(groups, capacity, PAGE * page_width), 'gr...  68.6 us
    all_gather x1, waiting for transfers between devices, per_device(): kv_all = lax.all_gather(kv_rows, 'm', axis=0, tiled=False)  33.6 us
    unnamed x20, local copies, waits for them, and re-layouts  10.7 us
    all_to_all x1, starting transfers between devices, per_device(): lax.all_to_all(out_slots.reshape(groups, capacity), 'grp', split_axis=0,...  10.1 us
    all_to_all x1, starting transfers between devices, per_device(): lax.all_to_all(outgoing.reshape(groups, capacity, PAGE * page_width), 'gr...  7.37 us
    dot_general x1, matrix products, per_device(): jnp.dot(chooser.astype(jnp.bfloat16), incoming.reshape(groups * capacity,...  4.79 us
  transfers between devices with their start and end apart: 3, of which 2 were waited for; matrix products, arithmetic and copies ran while one was open for 12% of the time, Pallas kernels for 0%

profile of v1, /device:TPU:1, one launch (start us, length us, event | category | flops | bytes accessed | tf_op | source)
XLA Modules:
  0.0 236.0 jit_solution(2786181492327652913)
XLA Ops:
  7.2 2.3 pad_maximum_fusion
  9.8 0.7 copy.36
  10.5 10.1 %all-to-all-start = ((s32[8,1,1]{2,1,0:T(1,128)}), s32[8,1,1]{2,1,0:T(1,128)S(1)}, u32[]{:S(2)}, u32[]{:S(2)}) async-start(s32[8,1,1]{2,1,0:T(1,128)} %copy.36), calls=%async_computation | async-start | bytes 8192 | tf_op jit(solution)/shard_map/all_to_all | solution.py:226
  20.6 2.0 concatenate.13
  22.6 0.6 constant_dynamic-slice_fusion
  23.2 0.7 compare_reduce_fusion
  23.9 0.2 broadcast_bitcast_fusion
  24.1 0.6 copy.46
  24.7 2.3 fusion
  27.1 0.5 broadcast.72
  27.5 3.8 %reduce.5 = bf16[8,131072]{1,0:T(8,128)(2,1)S(1)} reduce(bf16[8,1,131072]{2,0,1:T(8,128)(2,1)} %fusion, bf16[]{:T(256)} %broadcast.72), dimensions={1}, to_apply=%copy.37.reduce_sub_computation | reduce | bytes 4194306 | tf_op jit(solution)/shard_map/reshape | solution.py:220
  31.3 3.2 %reshape.163 = bf16[8,2,65536]{2,1,0:T(2,128)(2,1)} reshape(bf16[8,131072]{1,0:T(8,128)(2,1)S(1)} %reduce.5) | data formatting | bytes 4194304
  34.6 7.4 %all-to-all-start.1 = ((bf16[8,2,65536]{2,1,0:T(2,128)(2,1)}), bf16[8,2,65536]{2,1,0:T(2,128)(2,1)S(1)}, u32[]{:S(2)}, u32[]{:S(2)}) async-start(bf16[8,2,65536]{2,1,0:T(2,128)(2,1)} %reshape.163), calls=%async_computation.1 | async-start | bytes 4194304 | tf_op jit(solution)/shard_map/all_to_all | solution.py:219
  42.4 0.2 fusion.25
  42.8 0.3 fusion.5
  43.1 0.9 copy.38
  43.9 1.3 pad_add_fusion.refs_0_
  45.2 0.2 reduce.2
  45.4 68.6 %all-to-all-done.1 = bf16[8,2,65536]{2,1,0:T(2,128)(2,1)S(1)} async-done(((bf16[8,2,65536]{2,1,0:T(2,128)(2,1)}), bf16[8,2,65536]{2,1,0:T(2,128)(2,1)S(1)}, u32[]{:S(2)}, u32[]{:S(2)}) %all-to-all-start.1) | async-done | bytes 2097184 | tf_op jit(solution)/shard_map/all_to_all | solution.py:219
  114.0 4.4 %reshape.164 = bf16[8,1,131072]{2,1,0:T(2,128)(2,1)} reshape(bf16[8,2,65536]{2,1,0:T(2,128)(2,1)S(1)} %all-to-all-done.1) | data formatting | bytes 4194304
  118.5 4.8 %convolution_convert_fusion.1 = bf16[4,131072]{1,0:T(4,128)(2,1)S(1)} fusion(bf16[8,1,131072]{2,1,0:T(2,128)(2,1)} %reshape.164, s32[8]{0:T(128)S(1)} %reduce.2), kind=kOutput, calls=%fused_computation.2 | convolution fusion | flops 8912928 | bytes 3145760 | tf_op jit(solution)/shard_map/dot_general | solution.py:231
  123.3 1.3 copy.61
  124.5 33.6 %all-gather.3.cloned.1.call-done = bf16[4096,1024]{1,0:T(8,128)(2,1)} async-done(((bf16[512,1024]{1,0:T(8,128)(2,1)}), bf16[4096,1024]{1,0:T(8,128)(2,1)}) %all-gather.3.cloned.1.call-update) | async-done | bytes 8388624 | tf_op jit(solution)/shard_map/all_gather | solution.py:180
  158.1 71.0 %long_flash.1 = bf16[512,1024]{1,0:T(8,128)(2,1)} custom-call(s32[2]{0:T(128)} %pad_add_fusion.refs_0_, bf16[512,1024]{1,0:T(8,128)(2,1)} %bitcast.60, bf16[16,256,1024]{2,1,0:T(8,128)(2,1)} %bitcast.57, bf16[16,256,1024]{2,1,0:T(8,128)(2,1)} %bitcast.58), custom_call_target="tpu_custom_call" | custom-call | flops 4563402752 | bytes 11010048 | tf_op jit(solution)/shard_map/long_flash/pallas_call | solution.py:140
  (28 shorter events, 0.9 us)
Async XLA Ops:
  7.2 15.4 %copy-start = (s32[1,8]{1,0:T(1,128)S(1)}, s32[1,8]{1,0:T(1,128)}, u32[]{:S(2)}) copy-start(s32[1,8]{1,0:T(1,128)} %param.13) | copy-start | bytes 100
  7.2 2.4 %copy-start.5 = (s32[1,4]{1,0:T(1,128)S(1)}, s32[1,4]{1,0:T(1,128)}, u32[]{:S(2)}) copy-start(s32[1,4]{1,0:T(1,128)} %param.18) | copy-start | bytes 52
  7.2 2.6 %copy-start.6 = (s32[1,4]{1,0:T(1,128)S(1)}, s32[1,4]{1,0:T(1,128)}, u32[]{:S(2)}) copy-start(s32[1,4]{1,0:T(1,128)} %param.19) | copy-start | bytes 52
  7.2 150.9 %all-gather.3.cloned.1.call-start = ((), (), s32[]{:S(2)}) async-start(), calls=%async_computation.2 | async-start | bytes 9437184 | tf_op jit(solution)/shard_map/all_gather | solution.py:180
  10.5 24.1 %all-to-all-start = ((s32[8,1,1]{2,1,0:T(1,128)}), s32[8,1,1]{2,1,0:T(1,128)S(1)}, u32[]{:S(2)}, u32[]{:S(2)}) async-start(s32[8,1,1]{2,1,0:T(1,128)} %copy.36), calls=%async_computation | async-start | bytes 8192 | tf_op jit(solution)/shard_map/all_to_all | solution.py:226
  34.6 7.4 %copy-start.2 = (bf16[1,128,512]{2,1,0:T(8,128)(2,1)S(1)}, bf16[1,128,512]{2,1,0:T(8,128)(2,1)}, u32[]{:S(2)}) copy-start(bf16[1,128,512]{2,1,0:T(8,128)(2,1)} %param.16) | copy-start | bytes 393220
  34.6 7.5 %copy-start.1 = (bf16[1,128,1024]{2,1,0:T(8,128)(2,1)S(1)}, bf16[1,128,1024]{2,1,0:T(8,128)(2,1)}, u32[]{:S(2)}) copy-start(bf16[1,128,1024]{2,1,0:T(8,128)(2,1)} %param.14) | copy-start | bytes 786436
  34.6 7.7 %copy-start.3 = (bf16[1,128,512]{2,1,0:T(8,128)(2,1)S(1)}, bf16[1,128,512]{2,1,0:T(8,128)(2,1)}, u32[]{:S(2)}) copy-start(bf16[1,128,512]{2,1,0:T(8,128)(2,1)} %param.15) | copy-start | bytes 393220
  34.6 7.7 %copy-start.4 = (s32[1,1,128]{2,1,0:T(1,128)S(1)}, s32[1,1,128]{2,1,0:T(1,128)}, u32[]{:S(2)}) copy-start(s32[1,1,128]{2,1,0:T(1,128)} %param.17) | copy-start | bytes 1540
  34.6 79.4 %all-to-all-start.1 = ((bf16[8,2,65536]{2,1,0:T(2,128)(2,1)}), bf16[8,2,65536]{2,1,0:T(2,128)(2,1)S(1)}, u32[]{:S(2)}, u32[]{:S(2)}) async-start(bf16[8,2,65536]{2,1,0:T(2,128)(2,1)} %reshape.163), calls=%async_computation.1 | async-start | bytes 4194304 | tf_op jit(solution)/shard_map/all_to_all | solution.py:219
Sparse Core Ops, SparseCore 0:
  10.7 147.4 all-gather.2

commit v2 on v1

--- a/solution.py
+++ b/solution.py
@@ -60,13 +60,15 @@
     return jnp.transpose(result, (2, 0, 1, 3)).reshape(live_rows.shape[0], QUERY_HEADS * HEAD_SIZE)
 
 
-def flash_kernel(info_ref, q_ref, k_ref, v_ref, o_ref, m_sc, l_sc, acc_sc, *, block, blocks):
-    qb = pl.program_id(0)
-    kc = pl.program_id(1)
+def flash_kernel(info_ref, q_ref, k_ref, v_ref, o_ref, m_sc, l_sc, acc_sc, *, block):
+    step = pl.program_id(0)
     member = info_ref[0]
     length = info_ref[1]
-    bq = jnp.where(qb == 0, member, 2 * SPAN - 1 - member)
+    later = step > member
+    bq = jnp.where(later, 2 * SPAN - 1 - member, member)
+    kc = jnp.where(later, step - member - 1, step)
     kmax = jnp.minimum(bq, (length - 1) // block)
+    scale = 1.0 / math.sqrt(HEAD_SIZE)
 
     @pl.when(kc == 0)
     def _init():
@@ -74,12 +76,7 @@
         l_sc[...] = jnp.zeros(l_sc.shape, jnp.float32)
         acc_sc[...] = jnp.zeros(acc_sc.shape, jnp.float32)
 
-    @pl.when(kc <= kmax)
-    def _step():
-        q_pos = bq * block + lax.broadcasted_iota(jnp.int32, (block, block), 0)
-        k_pos = kc * block + lax.broadcasted_iota(jnp.int32, (block, block), 1)
-        visible = (k_pos <= q_pos) & (k_pos < length) & (q_pos < length)
-        scale = 1.0 / math.sqrt(HEAD_SIZE)
+    def attend(visible):
         for g in range(KEY_VALUE_HEADS):
             k = k_ref[0, :, g * HEAD_SIZE:(g + 1) * HEAD_SIZE]
             v = v_ref[0, :, g * HEAD_SIZE:(g + 1) * HEAD_SIZE]
@@ -89,11 +86,16 @@
                 s = lax.dot_general(
                     q, k, (((1,), (1,)), ((), ())), preferred_element_type=jnp.float32
                 ) * scale
-                s = jnp.where(visible, s, -jnp.inf)
+                if visible is not None:
+                    s = jnp.where(visible, s, -jnp.inf)
                 m_old = m_sc[h]
                 m_new = jnp.maximum(m_old, jnp.max(s, axis=-1, keepdims=True))
-                anchor = jnp.where(m_new > -jnp.inf, m_new, 0.0)
-                p = jnp.where(visible, jnp.exp(s - anchor), 0.0)
+                if visible is not None:
+                    anchor = jnp.where(m_new > -jnp.inf, m_new, 0.0)
+                    p = jnp.where(visible, jnp.exp(s - anchor), 0.0)
+                else:
+                    anchor = m_new
+                    p = jnp.exp(s - anchor)
                 alpha = jnp.exp(m_old - anchor)
                 l_sc[h] = alpha * l_sc[h] + jnp.sum(p, axis=-1, keepdims=True)
                 acc_sc[h] = alpha * acc_sc[h] + jnp.dot(
@@ -101,53 +103,73 @@
                 )
                 m_sc[h] = m_new
 
-    @pl.when(kc == blocks - 1)
+    edge = (kc == bq) | ((kc + 1) * block > length)
+
+    @pl.when((kc <= kmax) & edge)
+    def _edge_step():
+        q_pos = bq * block + lax.broadcasted_iota(jnp.int32, (block, block), 0)
+        k_pos = kc * block + lax.broadcasted_iota(jnp.int32, (block, block), 1)
+        attend((k_pos <= q_pos) & (k_pos < length))
+
+    @pl.when((kc <= kmax) & jnp.logical_not(edge))
+    def _full_step():
+        attend(None)
+
+    @pl.when(kc == bq)
     def _finish():
+        live = (bq * block + lax.broadcasted_iota(jnp.int32, (block, 1), 0)) < length
         for h in range(QUERY_HEADS):
             l = l_sc[h]
             divisor = jnp.where(l > 0, l, 1.0)
-            o_ref[:, h * HEAD_SIZE:(h + 1) * HEAD_SIZE] = (acc_sc[h] / divisor).astype(o_ref.dtype)
+            result = jnp.where(live, acc_sc[h] / divisor, 0.0)
+            o_ref[:, h * HEAD_SIZE:(h + 1) * HEAD_SIZE] = result.astype(o_ref.dtype)
 
 
 def long_attention(info, query_rows, kv_all, block):
-    blocks = 2 * SPAN
+    steps = 2 * SPAN + 1
     half_kv = kv_all.shape[-1] // 2
-
-    def kv_index(qb, kc, info_ref, which):
+    x_size = SPAN // 2
+
+    def q_index(step, info_ref):
+        return (jnp.where(step > info_ref[0], 1, 0), 0)
+
+    def kv_index(step, info_ref, which):
         member = info_ref[0]
         length = info_ref[1]
-        bq = jnp.where(qb == 0, member, 2 * SPAN - 1 - member)
+        later = step > member
+        bq = jnp.where(later, 2 * SPAN - 1 - member, member)
+        kc = jnp.where(later, step - member - 1, step)
         kk = jnp.minimum(kc, jnp.minimum(bq, (length - 1) // block))
-        j = jnp.where(kk < SPAN, 2 * kk, 2 * (2 * SPAN - 1 - kk) + 1)
+        source = jnp.where(kk < SPAN, kk, 2 * SPAN - 1 - kk)
+        half = jnp.where(kk < SPAN, 0, 1)
+        j = (source % x_size) * 4 + (source // x_size) * 2 + half
         return (j, 0, which)
 
     grid_spec = pltpu.PrefetchScalarGridSpec(
         num_scalar_prefetch=1,
-        grid=(2, blocks),
+        grid=(steps,),
         in_specs=[
-            pl.BlockSpec((block, query_rows.shape[1]), lambda qb, kc, info_ref: (qb, 0)),
-            pl.BlockSpec((1, block, half_kv), lambda qb, kc, info_ref: kv_index(qb, kc, info_ref, 0)),
-            pl.BlockSpec((1, block, half_kv), lambda qb, kc, info_ref: kv_index(qb, kc, info_ref, 1)),
+            pl.BlockSpec((block, query_rows.shape[1]), q_index),
+            pl.BlockSpec((1, block, half_kv), lambda step, info_ref: kv_index(step, info_ref, 0)),
+            pl.BlockSpec((1, block, half_kv), lambda step, info_ref: kv_index(step, info_ref, 1)),
         ],
-        out_specs=pl.BlockSpec((block, query_rows.shape[1]), lambda qb, kc, info_ref: (qb, 0)),
+        out_specs=pl.BlockSpec((block, query_rows.shape[1]), q_index),
         scratch_shapes=[
             pltpu.VMEM((QUERY_HEADS, block, 1), jnp.float32),
             pltpu.VMEM((QUERY_HEADS, block, 1), jnp.float32),
             pltpu.VMEM((QUERY_HEADS, block, HEAD_SIZE), jnp.float32),
         ],
     )
-    flops = 4 * 17 * block * block * HEAD_SIZE * QUERY_HEADS
+    flops = 4 * steps * block * block * HEAD_SIZE * QUERY_HEADS
     return pl.pallas_call(
-        lambda *refs: flash_kernel(*refs, block=block, blocks=blocks),
+        lambda *refs: flash_kernel(*refs, block=block),
         grid_spec=grid_spec,
         out_shape=jax.ShapeDtypeStruct(query_rows.shape, jnp.bfloat16),
-        compiler_params=pltpu.CompilerParams(
-            dimension_semantics=("arbitrary", "arbitrary"),
-        ),
+        compiler_params=pltpu.CompilerParams(dimension_semantics=("arbitrary",)),
         cost_estimate=pl.CostEstimate(
             flops=flops,
-            transcendentals=17 * block * block * QUERY_HEADS,
-            bytes_accessed=2 * query_rows.size * 2 + 17 * block * kv_all.shape[-1] * 2,
+            transcendentals=steps * block * block * QUERY_HEADS,
+            bytes_accessed=2 * query_rows.size * 2 + steps * block * kv_all.shape[-1] * 2,
         ),
         name="long_flash",
     )(info, query_rows, kv_all, kv_all)
@@ -166,7 +188,7 @@
     page_slot,
 ):
     half_rows = query_long.shape[1] // 2
-    member = lax.axis_index("m")
+    member = lax.axis_index("yl") * lax.axis_size("xx") + lax.axis_index("xx")
     group_id = lax.axis_index("r")
     length = lax.dynamic_index_in_dim(long_length[0], group_id, 0, keepdims=False)
     offsets = jnp.arange(half_rows, dtype=jnp.int32)
@@ -177,7 +199,8 @@
     value_row_block = long_prompt_values[0]
     kv_rows = jnp.concatenate([key_row_block, value_row_block], axis=-1)
 
-    kv_all = lax.all_gather(kv_rows, "m", axis=0, tiled=False)
+    kv_pair = lax.all_gather(kv_rows, "yl", axis=0, tiled=False)
+    kv_all = lax.all_gather(kv_pair, "xx", axis=0, tiled=False)
     kv_all = kv_all.reshape(2 * SPAN, half_rows, kv_rows.shape[-1])
     info = jnp.stack([member, length]).astype(jnp.int32)
     long_out = long_attention(info, query_long[0], kv_all, half_rows)
@@ -244,8 +267,10 @@
     n_grp = mesh.shape["grp"]
     n_cp = mesh.shape["cp"]
     stride = n_cp // SPAN
-    split_mesh = Mesh(mesh.devices.reshape(n_grp, SPAN, stride), ("grp", "m", "r"))
-    rows = ("m", "r")
+    split_mesh = Mesh(
+        mesh.devices.reshape(n_grp, 2, SPAN // 2, stride), ("grp", "yl", "xx", "r")
+    )
+    rows = ("yl", "xx", "r")
     in_specs = (
         P("grp", rows, None),
         P("grp", rows, None),

time: 239 us -> 220 us (0.921); the launches traced: 236 us -> 220 us
  Pallas kernels: 71 us -> 65.2 us
  waiting for transfers between devices: 102 us -> 96.3 us
  starting transfers between devices: 17.5 us -> 14.1 us
    all_to_all x1, waiting for transfers between devices: 68.6 us -> 33.4 us  [per_device(): lax.all_to_all(outgoing.reshape(groups, capacity, PAGE * page_width), 'gr...]
    all_gather x1 -> x2, waiting for transfers between devices: 33.6 us -> 62.9 us  [the longest x1 47.4 us: per_device(): kv_pair = lax.all_gather(kv_rows, 'yl', axis=0, tiled=False)]
    pallas_call x1, Pallas kernels: 71 us -> 65.2 us  [long_attention(): pl.pallas_call(lambda *refs: flash_kernel(*refs, block=block), grid_spec=...]
    all_to_all x1, starting transfers between devices: 10.1 us -> 6.67 us  [per_device(): lax.all_to_all(out_slots.reshape(groups, capacity), 'grp', split_axis=0,...]
    unnamed x20 -> x22, local copies, waits for them, and re-layouts: 10.7 us -> 10.7 us
  transfers between devices with their start and end apart: 3 -> 4, of which waited for: 2 -> 3; matrix products, arithmetic and copies ran while one was open for 12% -> 13% of each run, Pallas kernels for 0% -> 0%
where the time goes in v2:
time: 220 us
  waiting for transfers between devices  96.3 us (44%)
  Pallas kernels  65.2 us (30%)
  between operations  14.2 us (6%)
  starting transfers between devices  14.1 us (6%)
  local copies, waits for them, and re-layouts  13.6 us (6%)
  other arithmetic  8.86 us (4%)
  matrix products  7.64 us (3%)
    pallas_call x1, Pallas kernels, long_attention(): pl.pallas_call(lambda *refs: flash_kernel(*refs, block=block), grid_spec=...  65.2 us
    all_gather x1, waiting for transfers between devices, per_device(): kv_pair = lax.all_gather(kv_rows, 'yl', axis=0, tiled=False)  47.4 us
    all_to_all x1, waiting for transfers between devices, per_device(): lax.all_to_all(outgoing.reshape(groups, capacity, PAGE * page_width), 'gr...  33.4 us
    all_gather x1, waiting for transfers between devices, per_device(): kv_all = lax.all_gather(kv_pair, 'xx', axis=0, tiled=False)  15.5 us
    unnamed x22, local copies, waits for them, and re-layouts  10.7 us
    all_to_all x1, starting transfers between devices, per_device(): lax.all_to_all(outgoing.reshape(groups, capacity, PAGE * page_width), 'gr...  7.35 us
    all_to_all x1, starting transfers between devices, per_device(): lax.all_to_all(out_slots.reshape(groups, capacity), 'grp', split_axis=0,...  6.67 us
    dot_general x1, matrix products, per_device(): jnp.dot(chooser.astype(jnp.bfloat16), incoming.reshape(groups * capacity,...  4.8 us
  transfers between devices with their start and end apart: 4, of which 3 were waited for; matrix products, arithmetic and copies ran while one was open for 13% of the time, Pallas kernels for 0%

profile of v2, /device:TPU:1, one launch (start us, length us, event | category | flops | bytes accessed | tf_op | source)
XLA Modules:
  0.0 219.9 jit_solution(5822379137541589481)
XLA Ops:
  7.2 2.3 %pad_maximum_fusion = bf16[512,1024]{1,0:T(8,128)(2,1)} fusion(bf16[512,512]{1,0:T(8,128)(2,1)} %bitcast.65, bf16[512,512]{1,0:T(8,128)(2,1)} %bitcast.66), kind=kLoop, calls=%fused_computation.12 | loop fusion | flops 2097152 | bytes 2097152 | tf_op jit(solution)/shard_map/concatenate | solution.py:200
  9.6 47.4 %all-gather.5.cloned.1.call-done = bf16[1024,1024]{1,0:T(8,128)(2,1)} async-done(((bf16[512,1024]{1,0:T(8,128)(2,1)}), bf16[1024,1024]{1,0:T(8,128)(2,1)}) %all-gather.5.cloned.1.call-update) | async-done | bytes 2097168 | tf_op jit(solution)/shard_map/all_gather | solution.py:202
  57.3 0.7 copy.36
  58.0 6.7 %all-to-all-start = ((s32[8,1,1]{2,1,0:T(1,128)}), s32[8,1,1]{2,1,0:T(1,128)S(1)}, u32[]{:S(2)}, u32[]{:S(2)}) async-start(s32[8,1,1]{2,1,0:T(1,128)} %copy.36), calls=%async_computation | async-start | bytes 8192 | tf_op jit(solution)/shard_map/all_to_all | solution.py:249
  64.6 0.8 concatenate.13
  65.4 0.6 constant_dynamic-slice_fusion
  66.0 0.7 compare_reduce_fusion
  66.9 0.6 copy.46
  67.6 2.3 %fusion = bf16[8,1,131072]{2,0,1:T(8,128)(2,1)} fusion(pred[4,131072]{1,0:T(4,128)(4,1)S(1)} %bitcast.64, bf16[4,131072]{1,0:T(4,128)(2,1)S(1)} %concatenate.13, s32[4]{0:T(128)S(1)} %fusion.22), kind=kOutput, calls=%fused_computation.1 | convolution fusion | flops 9961504 | bytes 3670032 | tf_op jit(solution)/shard_map/dot_general | solution.py:237
  69.9 0.6 broadcast.72
  70.5 3.9 %reduce.5 = bf16[8,131072]{1,0:T(8,128)(2,1)S(1)} reduce(bf16[8,1,131072]{2,0,1:T(8,128)(2,1)} %fusion, bf16[]{:T(256)} %broadcast.72), dimensions={1}, to_apply=%copy.37.reduce_sub_computation | reduce | bytes 4194306 | tf_op jit(solution)/shard_map/reshape | solution.py:243
  74.4 3.2 %reshape.164 = bf16[8,2,65536]{2,1,0:T(2,128)(2,1)} reshape(bf16[8,131072]{1,0:T(8,128)(2,1)S(1)} %reduce.5) | data formatting | bytes 4194304
  77.7 7.3 %all-to-all-start.1 = ((bf16[8,2,65536]{2,1,0:T(2,128)(2,1)}), bf16[8,2,65536]{2,1,0:T(2,128)(2,1)S(1)}, u32[]{:S(2)}, u32[]{:S(2)}) async-start(bf16[8,2,65536]{2,1,0:T(2,128)(2,1)} %reshape.164), calls=%async_computation.1 | async-start | bytes 4194304 | tf_op jit(solution)/shard_map/all_to_all | solution.py:242
  85.5 0.2 fusion.25
  85.9 0.3 fusion.5
  86.1 0.9 copy.38
  87.0 1.3 pad_add_fusion.refs_0_
  88.3 0.2 reduce.2
  88.5 33.4 %all-to-all-done.1 = bf16[8,2,65536]{2,1,0:T(2,128)(2,1)S(1)} async-done(((bf16[8,2,65536]{2,1,0:T(2,128)(2,1)}), bf16[8,2,65536]{2,1,0:T(2,128)(2,1)S(1)}, u32[]{:S(2)}, u32[]{:S(2)}) %all-to-all-start.1) | async-done | bytes 2097184 | tf_op jit(solution)/shard_map/all_to_all | solution.py:242
  121.9 4.4 %reshape.165 = bf16[8,1,131072]{2,1,0:T(2,128)(2,1)} reshape(bf16[8,2,65536]{2,1,0:T(2,128)(2,1)S(1)} %all-to-all-done.1) | data formatting | bytes 4194304
  126.3 4.8 %convolution_convert_fusion.1 = bf16[4,131072]{1,0:T(4,128)(2,1)S(1)} fusion(bf16[8,1,131072]{2,1,0:T(2,128)(2,1)} %reshape.165, s32[8]{0:T(128)S(1)} %reduce.2), kind=kOutput, calls=%fused_computation.2 | convolution fusion | flops 8912928 | bytes 3145760 | tf_op jit(solution)/shard_map/dot_general | solution.py:254
  131.1 1.3 copy.61
  132.4 15.5 %all-gather.7.cloned.1.call-done = bf16[8,512,1024]{2,1,0:T(8,128)(2,1)} async-done(((bf16[2,512,1024]{2,1,0:T(8,128)(2,1)}), bf16[8,512,1024]{2,1,0:T(8,128)(2,1)}) %all-gather.7.cloned.1.call-update) | async-done | bytes 8388624 | tf_op jit(solution)/shard_map/all_gather | solution.py:203
  147.9 65.2 %long_flash.1 = bf16[512,1024]{1,0:T(8,128)(2,1)} custom-call(s32[2]{0:T(128)} %pad_add_fusion.refs_0_, bf16[512,1024]{1,0:T(8,128)(2,1)} %bitcast.62, bf16[16,256,1024]{2,1,0:T(8,128)(2,1)} %bitcast.58, bf16[16,256,1024]{2,1,0:T(8,128)(2,1)} %bitcast.59), custom_call_target="tpu_custom_call" | custom-call | flops 4563402752 | bytes 11010048 | tf_op jit(solution)/shard_map/long_flash/pallas_call | solution.py:164
  (33 shorter events, 1.2 us)
Async XLA Ops:
  7.2 58.3 %copy-start = (s32[1,8]{1,0:T(1,128)S(1)}, s32[1,8]{1,0:T(1,128)}, u32[]{:S(2)}) copy-start(s32[1,8]{1,0:T(1,128)} %param.13) | copy-start | bytes 100
  7.2 49.8 %all-gather.5.cloned.1.call-start = ((), (), s32[]{:S(2)}) async-start(), calls=%async_computation.2 | async-start | bytes 3145728 | tf_op jit(solution)/shard_map/all_gather | solution.py:202
  9.5 47.5 %copy-start.6 = (s32[1,4]{1,0:T(1,128)S(1)}, s32[1,4]{1,0:T(1,128)}, u32[]{:S(2)}) copy-start(s32[1,4]{1,0:T(1,128)} %param.18) | copy-start | bytes 52
  9.5 47.7 %copy-start.7 = (s32[1,4]{1,0:T(1,128)S(1)}, s32[1,4]{1,0:T(1,128)}, u32[]{:S(2)}) copy-start(s32[1,4]{1,0:T(1,128)} %param.19) | copy-start | bytes 52
  9.5 55.1 %copy-start.1 = (bf16[512,1024]{1,0:T(8,128)(2,1)S(1)}, bf16[512,1024]{1,0:T(8,128)(2,1)}, u32[]{:S(2)}) copy-start(bf16[512,1024]{1,0:T(8,128)(2,1)} %pad_maximum_fusion) | copy-start | bytes 3145732
  9.5 138.4 %all-gather.7.cloned.1.call-start = ((), (), s32[]{:S(2)}) async-start(), calls=%async_computation.3 | async-start | bytes 10485760 | tf_op jit(solution)/shard_map/all_gather | solution.py:203
  58.0 19.7 %all-to-all-start = ((s32[8,1,1]{2,1,0:T(1,128)}), s32[8,1,1]{2,1,0:T(1,128)S(1)}, u32[]{:S(2)}, u32[]{:S(2)}) async-start(s32[8,1,1]{2,1,0:T(1,128)} %copy.36), calls=%async_computation | async-start | bytes 8192 | tf_op jit(solution)/shard_map/all_to_all | solution.py:249
  77.6 7.4 %copy-start.3 = (bf16[1,128,512]{2,1,0:T(8,128)(2,1)S(1)}, bf16[1,128,512]{2,1,0:T(8,128)(2,1)}, u32[]{:S(2)}) copy-start(bf16[1,128,512]{2,1,0:T(8,128)(2,1)} %param.16) | copy-start | bytes 393220
  77.6 7.5 %copy-start.2 = (bf16[1,128,1024]{2,1,0:T(8,128)(2,1)S(1)}, bf16[1,128,1024]{2,1,0:T(8,128)(2,1)}, u32[]{:S(2)}) copy-start(bf16[1,128,1024]{2,1,0:T(8,128)(2,1)} %param.14) | copy-start | bytes 786436
  77.6 7.7 %copy-start.4 = (bf16[1,128,512]{2,1,0:T(8,128)(2,1)S(1)}, bf16[1,128,512]{2,1,0:T(8,128)(2,1)}, u32[]{:S(2)}) copy-start(bf16[1,128,512]{2,1,0:T(8,128)(2,1)} %param.15) | copy-start | bytes 393220
  77.6 7.7 %copy-start.5 = (s32[1,1,128]{2,1,0:T(1,128)S(1)}, s32[1,1,128]{2,1,0:T(1,128)}, u32[]{:S(2)}) copy-start(s32[1,1,128]{2,1,0:T(1,128)} %param.17) | copy-start | bytes 1540
  77.7 44.2 %all-to-all-start.1 = ((bf16[8,2,65536]{2,1,0:T(2,128)(2,1)}), bf16[8,2,65536]{2,1,0:T(2,128)(2,1)S(1)}, u32[]{:S(2)}, u32[]{:S(2)}) async-start(bf16[8,2,65536]{2,1,0:T(2,128)(2,1)} %reshape.164), calls=%async_computation.1 | async-start | bytes 4194304 | tf_op jit(solution)/shard_map/all_to_all | solution.py:242
Sparse Core Ops, SparseCore 0:
  10.7 46.2 all-gather.4
  59.1 88.7 all-gather.6

commit v3 on v2

--- a/solution.py
+++ b/solution.py
@@ -76,32 +76,39 @@
         l_sc[...] = jnp.zeros(l_sc.shape, jnp.float32)
         acc_sc[...] = jnp.zeros(acc_sc.shape, jnp.float32)
 
+    per_group = QUERY_HEADS // KEY_VALUE_HEADS
+    lane_tiles = block // HEAD_SIZE
+
     def attend(visible):
         for g in range(KEY_VALUE_HEADS):
             k = k_ref[0, :, g * HEAD_SIZE:(g + 1) * HEAD_SIZE]
             v = v_ref[0, :, g * HEAD_SIZE:(g + 1) * HEAD_SIZE]
-            for jj in range(QUERY_HEADS // KEY_VALUE_HEADS):
-                h = g * (QUERY_HEADS // KEY_VALUE_HEADS) + jj
-                q = q_ref[:, h * HEAD_SIZE:(h + 1) * HEAD_SIZE]
-                s = lax.dot_general(
-                    q, k, (((1,), (1,)), ((), ())), preferred_element_type=jnp.float32
-                ) * scale
-                if visible is not None:
-                    s = jnp.where(visible, s, -jnp.inf)
-                m_old = m_sc[h]
-                m_new = jnp.maximum(m_old, jnp.max(s, axis=-1, keepdims=True))
-                if visible is not None:
-                    anchor = jnp.where(m_new > -jnp.inf, m_new, 0.0)
-                    p = jnp.where(visible, jnp.exp(s - anchor), 0.0)
-                else:
-                    anchor = m_new
-                    p = jnp.exp(s - anchor)
-                alpha = jnp.exp(m_old - anchor)
-                l_sc[h] = alpha * l_sc[h] + jnp.sum(p, axis=-1, keepdims=True)
-                acc_sc[h] = alpha * acc_sc[h] + jnp.dot(
-                    p.astype(jnp.bfloat16), v, preferred_element_type=jnp.float32
-                )
-                m_sc[h] = m_new
+            q = jnp.concatenate(
+                [
+                    q_ref[:, (g * per_group + jj) * HEAD_SIZE:(g * per_group + jj + 1) * HEAD_SIZE]
+                    for jj in range(per_group)
+                ],
+                axis=0,
+            )
+            s = lax.dot_general(
+                q, k, (((1,), (1,)), ((), ())), preferred_element_type=jnp.float32
+            ) * scale
+            if visible is not None:
+                s = jnp.where(visible, s, -jnp.inf)
+            m_old = m_sc[g]
+            m_new = jnp.maximum(m_old, jnp.max(s, axis=-1, keepdims=True))
+            if visible is not None:
+                anchor = jnp.where(m_new > -jnp.inf, m_new, 0.0)
+                p = jnp.where(visible, jnp.exp(s - jnp.concatenate([anchor] * lane_tiles, axis=1)), 0.0)
+            else:
+                anchor = m_new
+                p = jnp.exp(s - jnp.concatenate([anchor] * lane_tiles, axis=1))
+            alpha = jnp.exp(m_old - anchor)
+            l_sc[g] = alpha * l_sc[g] + jnp.sum(p, axis=-1, keepdims=True)
+            acc_sc[g] = alpha * acc_sc[g] + jnp.dot(
+                p.astype(jnp.bfloat16), v, preferred_element_type=jnp.float32
+            )
+            m_sc[g] = m_new
 
     edge = (kc == bq) | ((kc + 1) * block > length)
 
@@ -109,7 +116,8 @@
     def _edge_step():
         q_pos = bq * block + lax.broadcasted_iota(jnp.int32, (block, block), 0)
         k_pos = kc * block + lax.broadcasted_iota(jnp.int32, (block, block), 1)
-        attend((k_pos <= q_pos) & (k_pos < length))
+        visible = (k_pos <= q_pos) & (k_pos < length)
+        attend(jnp.concatenate([visible] * per_group, axis=0))
 
     @pl.when((kc <= kmax) & jnp.logical_not(edge))
     def _full_step():
@@ -118,11 +126,16 @@
     @pl.when(kc == bq)
     def _finish():
         live = (bq * block + lax.broadcasted_iota(jnp.int32, (block, 1), 0)) < length
-        for h in range(QUERY_HEADS):
-            l = l_sc[h]
+        for g in range(KEY_VALUE_HEADS):
+            l = l_sc[g]
             divisor = jnp.where(l > 0, l, 1.0)
-            result = jnp.where(live, acc_sc[h] / divisor, 0.0)
-            o_ref[:, h * HEAD_SIZE:(h + 1) * HEAD_SIZE] = result.astype(o_ref.dtype)
+            result = acc_sc[g] / divisor
+            for jj in range(per_group):
+                h = g * per_group + jj
+                rows = result[jj * block:(jj + 1) * block]
+                o_ref[:, h * HEAD_SIZE:(h + 1) * HEAD_SIZE] = jnp.where(live, rows, 0.0).astype(
+                    o_ref.dtype
+                )
 
 
 def long_attention(info, query_rows, kv_all, block):
@@ -155,9 +168,9 @@
         ],
         out_specs=pl.BlockSpec((block, query_rows.shape[1]), q_index),
         scratch_shapes=[
-            pltpu.VMEM((QUERY_HEADS, block, 1), jnp.float32),
-            pltpu.VMEM((QUERY_HEADS, block, 1), jnp.float32),
-            pltpu.VMEM((QUERY_HEADS, block, HEAD_SIZE), jnp.float32),
+            pltpu.VMEM((KEY_VALUE_HEADS, QUERY_HEADS // KEY_VALUE_HEADS * block, HEAD_SIZE), jnp.float32),
+            pltpu.VMEM((KEY_VALUE_HEADS, QUERY_HEADS // KEY_VALUE_HEADS * block, HEAD_SIZE), jnp.float32),
+            pltpu.VMEM((KEY_VALUE_HEADS, QUERY_HEADS // KEY_VALUE_HEADS * block, HEAD_SIZE), jnp.float32),
         ],
     )
     flops = 4 * steps * block * block * HEAD_SIZE * QUERY_HEADS

time: 220 us -> 180 us (0.82); the launches traced: 220 us -> 177 us
  Pallas kernels: 65.2 us -> 21.9 us
    pallas_call x1, Pallas kernels: 65.2 us -> 21.9 us  [long_attention(): pl.pallas_call(lambda *refs: flash_kernel(*refs, block=block), grid_spec=...]
  transfers between devices with their start and end apart: 4 -> 4, of which waited for: 3 -> 3; matrix products, arithmetic and copies ran while one was open for 13% -> 16% of each run, Pallas kernels for 0% -> 0%
where the time goes in v3:
time: 180 us; the launch traced here: 177 us
  waiting for transfers between devices  96.3 us (54%)
  Pallas kernels  21.9 us (12%)
  between operations  14.2 us (8%)
  starting transfers between devices  14.1 us (8%)
  local copies, waits for them, and re-layouts  13.6 us (8%)
  other arithmetic  8.86 us (5%)
  matrix products  7.64 us (4%)
    all_gather x1, waiting for transfers between devices, per_device(): kv_pair = lax.all_gather(kv_rows, 'yl', axis=0, tiled=False)  47.4 us
    all_to_all x1, waiting for transfers between devices, per_device(): lax.all_to_all(outgoing.reshape(groups, capacity, PAGE * page_width), 'gr...  33.4 us
    pallas_call x1, Pallas kernels, long_attention(): pl.pallas_call(lambda *refs: flash_kernel(*refs, block=block), grid_spec=...  21.9 us
    all_gather x1, waiting for transfers between devices, per_device(): kv_all = lax.all_gather(kv_pair, 'xx', axis=0, tiled=False)  15.5 us
    unnamed x22, local copies, waits for them, and re-layouts  10.7 us
    all_to_all x1, starting transfers between devices, per_device(): lax.all_to_all(outgoing.reshape(groups, capacity, PAGE * page_width), 'gr...  7.35 us
    all_to_all x1, starting transfers between devices, per_device(): lax.all_to_all(out_slots.reshape(groups, capacity), 'grp', split_axis=0,...  6.67 us
    dot_general x1, matrix products, per_device(): jnp.dot(chooser.astype(jnp.bfloat16), incoming.reshape(groups * capacity,...  4.8 us
  transfers between devices with their start and end apart: 4, of which 3 were waited for; matrix products, arithmetic and copies ran while one was open for 16% of the time, Pallas kernels for 0%

profile of v3, /device:TPU:1, one launch (start us, length us, event | category | flops | bytes accessed | tf_op | source)
XLA Modules:
  0.0 176.7 jit_solution(2608271590252516321)
XLA Ops:
  7.2 2.3 %pad_maximum_fusion = bf16[512,1024]{1,0:T(8,128)(2,1)} fusion(bf16[512,512]{1,0:T(8,128)(2,1)} %bitcast.65, bf16[512,512]{1,0:T(8,128)(2,1)} %bitcast.66), kind=kLoop, calls=%fused_computation.12 | loop fusion | flops 2097152 | bytes 2097152 | tf_op jit(solution)/shard_map/concatenate | solution.py:213
  9.6 47.4 %all-gather.5.cloned.1.call-done = bf16[1024,1024]{1,0:T(8,128)(2,1)} async-done(((bf16[512,1024]{1,0:T(8,128)(2,1)}), bf16[1024,1024]{1,0:T(8,128)(2,1)}) %all-gather.5.cloned.1.call-update) | async-done | bytes 2097168 | tf_op jit(solution)/shard_map/all_gather | solution.py:215
  57.3 0.7 copy.36
  58.0 6.7 %all-to-all-start = ((s32[8,1,1]{2,1,0:T(1,128)}), s32[8,1,1]{2,1,0:T(1,128)S(1)}, u32[]{:S(2)}, u32[]{:S(2)}) async-start(s32[8,1,1]{2,1,0:T(1,128)} %copy.36), calls=%async_computation | async-start | bytes 8192 | tf_op jit(solution)/shard_map/all_to_all | solution.py:262
  64.6 0.8 concatenate.13
  65.4 0.6 constant_dynamic-slice_fusion
  66.0 0.7 compare_reduce_fusion
  66.9 0.6 copy.46
  67.6 2.3 %fusion = bf16[8,1,131072]{2,0,1:T(8,128)(2,1)} fusion(pred[4,131072]{1,0:T(4,128)(4,1)S(1)} %bitcast.64, bf16[4,131072]{1,0:T(4,128)(2,1)S(1)} %concatenate.13, s32[4]{0:T(128)S(1)} %fusion.22), kind=kOutput, calls=%fused_computation.1 | convolution fusion | flops 9961504 | bytes 3670032 | tf_op jit(solution)/shard_map/dot_general | solution.py:250
  69.9 0.6 broadcast.72
  70.5 3.9 %reduce.5 = bf16[8,131072]{1,0:T(8,128)(2,1)S(1)} reduce(bf16[8,1,131072]{2,0,1:T(8,128)(2,1)} %fusion, bf16[]{:T(256)} %broadcast.72), dimensions={1}, to_apply=%copy.37.reduce_sub_computation | reduce | bytes 4194306 | tf_op jit(solution)/shard_map/reshape | solution.py:256
  74.4 3.2 %reshape.164 = bf16[8,2,65536]{2,1,0:T(2,128)(2,1)} reshape(bf16[8,131072]{1,0:T(8,128)(2,1)S(1)} %reduce.5) | data formatting | bytes 4194304
  77.7 7.3 %all-to-all-start.1 = ((bf16[8,2,65536]{2,1,0:T(2,128)(2,1)}), bf16[8,2,65536]{2,1,0:T(2,128)(2,1)S(1)}, u32[]{:S(2)}, u32[]{:S(2)}) async-start(bf16[8,2,65536]{2,1,0:T(2,128)(2,1)} %reshape.164), calls=%async_computation.1 | async-start | bytes 4194304 | tf_op jit(solution)/shard_map/all_to_all | solution.py:255
  85.5 0.2 fusion.25
  85.9 0.3 fusion.5
  86.1 0.9 copy.38
  87.0 1.3 pad_add_fusion.refs_0_
  88.3 0.2 reduce.2
  88.5 33.4 %all-to-all-done.1 = bf16[8,2,65536]{2,1,0:T(2,128)(2,1)S(1)} async-done(((bf16[8,2,65536]{2,1,0:T(2,128)(2,1)}), bf16[8,2,65536]{2,1,0:T(2,128)(2,1)S(1)}, u32[]{:S(2)}, u32[]{:S(2)}) %all-to-all-start.1) | async-done | bytes 2097184 | tf_op jit(solution)/shard_map/all_to_all | solution.py:255
  121.9 4.4 %reshape.165 = bf16[8,1,131072]{2,1,0:T(2,128)(2,1)} reshape(bf16[8,2,65536]{2,1,0:T(2,128)(2,1)S(1)} %all-to-all-done.1) | data formatting | bytes 4194304
  126.3 4.8 %convolution_convert_fusion.1 = bf16[4,131072]{1,0:T(4,128)(2,1)S(1)} fusion(bf16[8,1,131072]{2,1,0:T(2,128)(2,1)} %reshape.165, s32[8]{0:T(128)S(1)} %reduce.2), kind=kOutput, calls=%fused_computation.2 | convolution fusion | flops 8912928 | bytes 3145760 | tf_op jit(solution)/shard_map/dot_general | solution.py:267
  131.1 1.3 copy.61
  132.4 15.5 %all-gather.7.cloned.1.call-done = bf16[8,512,1024]{2,1,0:T(8,128)(2,1)} async-done(((bf16[2,512,1024]{2,1,0:T(8,128)(2,1)}), bf16[8,512,1024]{2,1,0:T(8,128)(2,1)}) %all-gather.7.cloned.1.call-update) | async-done | bytes 8388624 | tf_op jit(solution)/shard_map/all_gather | solution.py:216
  147.9 21.9 %long_flash.1 = bf16[512,1024]{1,0:T(8,128)(2,1)} custom-call(s32[2]{0:T(128)} %pad_add_fusion.refs_0_, bf16[512,1024]{1,0:T(8,128)(2,1)} %bitcast.62, bf16[16,256,1024]{2,1,0:T(8,128)(2,1)} %bitcast.58, bf16[16,256,1024]{2,1,0:T(8,128)(2,1)} %bitcast.59), custom_call_target="tpu_custom_call" | custom-call | flops 4563402752 | bytes 11010048 | tf_op jit(solution)/shard_map/long_flash/pallas_call | solution.py:177
  (33 shorter events, 1.2 us)
Async XLA Ops:
  7.2 58.3 %copy-start = (s32[1,8]{1,0:T(1,128)S(1)}, s32[1,8]{1,0:T(1,128)}, u32[]{:S(2)}) copy-start(s32[1,8]{1,0:T(1,128)} %param.13) | copy-start | bytes 100
  7.2 49.8 %all-gather.5.cloned.1.call-start = ((), (), s32[]{:S(2)}) async-start(), calls=%async_computation.2 | async-start | bytes 3145728 | tf_op jit(solution)/shard_map/all_gather | solution.py:215
  9.5 47.5 %copy-start.6 = (s32[1,4]{1,0:T(1,128)S(1)}, s32[1,4]{1,0:T(1,128)}, u32[]{:S(2)}) copy-start(s32[1,4]{1,0:T(1,128)} %param.18) | copy-start | bytes 52
  9.5 47.7 %copy-start.7 = (s32[1,4]{1,0:T(1,128)S(1)}, s32[1,4]{1,0:T(1,128)}, u32[]{:S(2)}) copy-start(s32[1,4]{1,0:T(1,128)} %param.19) | copy-start | bytes 52
  9.5 55.1 %copy-start.1 = (bf16[512,1024]{1,0:T(8,128)(2,1)S(1)}, bf16[512,1024]{1,0:T(8,128)(2,1)}, u32[]{:S(2)}) copy-start(bf16[512,1024]{1,0:T(8,128)(2,1)} %pad_maximum_fusion) | copy-start | bytes 3145732
  9.5 138.4 %all-gather.7.cloned.1.call-start = ((), (), s32[]{:S(2)}) async-start(), calls=%async_computation.3 | async-start | bytes 10485760 | tf_op jit(solution)/shard_map/all_gather | solution.py:216
  58.0 19.7 %all-to-all-start = ((s32[8,1,1]{2,1,0:T(1,128)}), s32[8,1,1]{2,1,0:T(1,128)S(1)}, u32[]{:S(2)}, u32[]{:S(2)}) async-start(s32[8,1,1]{2,1,0:T(1,128)} %copy.36), calls=%async_computation | async-start | bytes 8192 | tf_op jit(solution)/shard_map/all_to_all | solution.py:262
  77.6 7.4 %copy-start.3 = (bf16[1,128,512]{2,1,0:T(8,128)(2,1)S(1)}, bf16[1,128,512]{2,1,0:T(8,128)(2,1)}, u32[]{:S(2)}) copy-start(bf16[1,128,512]{2,1,0:T(8,128)(2,1)} %param.16) | copy-start | bytes 393220
  77.6 7.5 %copy-start.2 = (bf16[1,128,1024]{2,1,0:T(8,128)(2,1)S(1)}, bf16[1,128,1024]{2,1,0:T(8,128)(2,1)}, u32[]{:S(2)}) copy-start(bf16[1,128,1024]{2,1,0:T(8,128)(2,1)} %param.14) | copy-start | bytes 786436
  77.6 7.7 %copy-start.4 = (bf16[1,128,512]{2,1,0:T(8,128)(2,1)S(1)}, bf16[1,128,512]{2,1,0:T(8,128)(2,1)}, u32[]{:S(2)}) copy-start(bf16[1,128,512]{2,1,0:T(8,128)(2,1)} %param.15) | copy-start | bytes 393220
  77.6 7.7 %copy-start.5 = (s32[1,1,128]{2,1,0:T(1,128)S(1)}, s32[1,1,128]{2,1,0:T(1,128)}, u32[]{:S(2)}) copy-start(s32[1,1,128]{2,1,0:T(1,128)} %param.17) | copy-start | bytes 1540
  77.7 44.2 %all-to-all-start.1 = ((bf16[8,2,65536]{2,1,0:T(2,128)(2,1)}), bf16[8,2,65536]{2,1,0:T(2,128)(2,1)S(1)}, u32[]{:S(2)}, u32[]{:S(2)}) async-start(bf16[8,2,65536]{2,1,0:T(2,128)(2,1)} %reshape.164), calls=%async_computation.1 | async-start | bytes 4194304 | tf_op jit(solution)/shard_map/all_to_all | solution.py:255
Sparse Core Ops, SparseCore 0:
  10.7 46.2 all-gather.4
  59.1 88.7 all-gather.6

commit v4 on v3

--- a/solution.py
+++ b/solution.py
@@ -155,7 +155,8 @@
         kk = jnp.minimum(kc, jnp.minimum(bq, (length - 1) // block))
         source = jnp.where(kk < SPAN, kk, 2 * SPAN - 1 - kk)
         half = jnp.where(kk < SPAN, 0, 1)
-        j = (source % x_size) * 4 + (source // x_size) * 2 + half
+        other_row = jnp.where(source // x_size == member // x_size, 0, 1)
+        j = (source % x_size) * 4 + other_row * 2 + half
         return (j, 0, which)
 
     grid_spec = pltpu.PrefetchScalarGridSpec(
@@ -212,7 +213,9 @@
     value_row_block = long_prompt_values[0]
     kv_rows = jnp.concatenate([key_row_block, value_row_block], axis=-1)
 
-    kv_pair = lax.all_gather(kv_rows, "yl", axis=0, tiled=False)
+    y_size = lax.axis_size("yl")
+    partner = lax.ppermute(kv_rows, "yl", [(i, (i + 1) % y_size) for i in range(y_size)])
+    kv_pair = jnp.stack([kv_rows, partner])
     kv_all = lax.all_gather(kv_pair, "xx", axis=0, tiled=False)
     kv_all = kv_all.reshape(2 * SPAN, half_rows, kv_rows.shape[-1])
     info = jnp.stack([member, length]).astype(jnp.int32)

time: 180 us -> 163 us (0.906); the launches traced: 177 us -> 162 us
  waiting for transfers between devices: 96.3 us -> 67.5 us
  starting transfers between devices: 14.1 us -> 24.7 us
  Pallas kernels: 21.9 us -> 24.6 us
    all_gather x1 -> x0, waiting for transfers between devices: 47.4 us -> none  [per_device(): kv_pair = lax.all_gather(kv_rows, 'yl', axis=0, tiled=False)]
    ppermute x0 -> x1, waiting for transfers between devices: none -> 18 us  [per_device(): lax.ppermute(kv_rows, 'yl', [(i, (i + 1) % y_size) for i in range(y_size)])]
    all_to_all x1, waiting for transfers between devices: 33.4 us -> 44.5 us  [per_device(): lax.all_to_all(outgoing.reshape(groups, capacity, PAGE * page_width), 'gr...]
    all_gather x1, waiting for transfers between devices: 15.5 us -> 5 us  [per_device(): kv_all = lax.all_gather(kv_pair, 'xx', axis=0, tiled=False)]
    all_to_all x1, starting transfers between devices: 6.67 us -> 13.3 us  [per_device(): lax.all_to_all(out_slots.reshape(groups, capacity), 'grp', split_axis=0,...]
    ppermute x0 -> x1, starting transfers between devices: none -> 4.02 us  [per_device(): lax.ppermute(kv_rows, 'yl', [(i, (i + 1) % y_size) for i in range(y_size)])]
    another operation x0 -> x2, other arithmetic: none -> 2.88 us  [per_device(): kv_pair = jnp.stack([kv_rows, partner])]
    pallas_call x1, Pallas kernels: 21.9 us -> 24.6 us  [long_attention(): pl.pallas_call(lambda *refs: flash_kernel(*refs, block=block), grid_spec=...]
  transfers between devices with their start and end apart: 4 -> 4, of which waited for: 3 -> 3; matrix products, arithmetic and copies ran while one was open for 16% -> 17% of each run, Pallas kernels for 0% -> 0%
where the time goes in v4:
time: 163 us; the launch traced here: 162 us
  waiting for transfers between devices  67.5 us (41%)
  starting transfers between devices  24.7 us (15%)
  Pallas kernels  24.6 us (15%)
  local copies, waits for them, and re-layouts  14.3 us (9%)
  between operations  14.2 us (9%)
  other arithmetic  9.46 us (6%)
  matrix products  7.56 us (5%)
    all_to_all x1, waiting for transfers between devices, per_device(): lax.all_to_all(outgoing.reshape(groups, capacity, PAGE * page_width), 'gr...  44.5 us
    pallas_call x1, Pallas kernels, long_attention(): pl.pallas_call(lambda *refs: flash_kernel(*refs, block=block), grid_spec=...  24.6 us
    ppermute x1, waiting for transfers between devices, per_device(): lax.ppermute(kv_rows, 'yl', [(i, (i + 1) % y_size) for i in range(y_size)])  18 us
    all_to_all x1, starting transfers between devices, per_device(): lax.all_to_all(out_slots.reshape(groups, capacity), 'grp', split_axis=0,...  13.3 us
    unnamed x20, local copies, waits for them, and re-layouts  11.3 us
    all_to_all x1, starting transfers between devices, per_device(): lax.all_to_all(outgoing.reshape(groups, capacity, PAGE * page_width), 'gr...  7.35 us
    all_gather x1, waiting for transfers between devices, per_device(): kv_all = lax.all_gather(kv_pair, 'xx', axis=0, tiled=False)  5 us
    dot_general x1, matrix products, per_device(): jnp.dot(chooser.astype(jnp.bfloat16), incoming.reshape(groups * capacity,...  4.71 us
  transfers between devices with their start and end apart: 4, of which 3 were waited for; matrix products, arithmetic and copies ran while one was open for 17% of the time, Pallas kernels for 0%

profile of v4, /device:TPU:1, one launch (start us, length us, event | category | flops | bytes accessed | tf_op | source)
XLA Modules:
  0.0 162.3 jit_solution(2839352885844048923)
XLA Ops:
  7.2 1.3 fusion.25
  8.6 4.0 %collective-permute-start = (bf16[512,1024]{1,0:T(8,128)(2,1)S(1)}, bf16[512,1024]{1,0:T(8,128)(2,1)S(1)}, u32[]{:S(2)}, u32[]{:S(2)}) collective-permute-start(bf16[512,1024]{1,0:T(8,128)(2,1)S(1)} %get-tuple-element.16), channel_id=1, source_target_pairs={{0,32},{32,0},{1,33},{33,1},{2,34},{34,2},{3,35},{35,3},{4,36},{36... | collective-permute-start | bytes 3145736 | tf_op jit(solution)/shard_map/ppermute | solution.py:217
  12.6 18.0 %collective-permute-done = bf16[512,1024]{1,0:T(8,128)(2,1)S(1)} collective-permute-done((bf16[512,1024]{1,0:T(8,128)(2,1)S(1)}, bf16[512,1024]{1,0:T(8,128)(2,1)S(1)}, u32[]{:S(2)}, u32[]{:S(2)}) %collective-permute-start) | collective-permute-done | bytes 1048608 | tf_op jit(solution)/shard_map/ppermute | solution.py:217
  30.6 1.5 pad_maximum_fusion
  32.2 0.6 copy-done.5
  33.1 0.7 copy.36
  33.8 13.3 %all-to-all-start = ((s32[8,1,1]{2,1,0:T(1,128)}), s32[8,1,1]{2,1,0:T(1,128)S(1)}, u32[]{:S(2)}, u32[]{:S(2)}) async-start(s32[8,1,1]{2,1,0:T(1,128)} %copy.36), calls=%async_computation | async-start | bytes 8192 | tf_op jit(solution)/shard_map/all_to_all | solution.py:265
  47.1 0.8 concatenate.13
  47.9 0.6 constant_dynamic-slice_fusion
  48.5 0.7 compare_reduce_fusion
  49.4 0.6 copy.46
  50.0 2.3 %fusion = bf16[8,1,131072]{2,0,1:T(8,128)(2,1)} fusion(pred[4,131072]{1,0:T(4,128)(4,1)S(1)} %bitcast.66, bf16[4,131072]{1,0:T(4,128)(2,1)S(1)} %concatenate.13, s32[4]{0:T(128)S(1)} %fusion.22), kind=kOutput, calls=%fused_computation.1 | convolution fusion | flops 9961504 | bytes 3670032 | tf_op jit(solution)/shard_map/dot_general | solution.py:253
  52.4 0.6 broadcast.72
  52.9 3.9 %reduce.5 = bf16[8,131072]{1,0:T(8,128)(2,1)S(1)} reduce(bf16[8,1,131072]{2,0,1:T(8,128)(2,1)} %fusion, bf16[]{:T(256)} %broadcast.72), dimensions={1}, to_apply=%copy.37.reduce_sub_computation | reduce | bytes 4194306 | tf_op jit(solution)/shard_map/reshape | solution.py:259
  56.8 3.2 %reshape.163 = bf16[8,2,65536]{2,1,0:T(2,128)(2,1)} reshape(bf16[8,131072]{1,0:T(8,128)(2,1)S(1)} %reduce.5) | data formatting | bytes 4194304
  60.1 7.3 %all-to-all-start.1 = ((bf16[8,2,65536]{2,1,0:T(2,128)(2,1)}), bf16[8,2,65536]{2,1,0:T(2,128)(2,1)S(1)}, u32[]{:S(2)}, u32[]{:S(2)}) async-start(bf16[8,2,65536]{2,1,0:T(2,128)(2,1)} %reshape.163), calls=%async_computation.1 | async-start | bytes 4194304 | tf_op jit(solution)/shard_map/all_to_all | solution.py:258
  68.6 0.9 copy.38
  69.4 1.3 pad_add_fusion.refs_0_
  71.0 44.5 %all-to-all-done.1 = bf16[8,2,65536]{2,1,0:T(2,128)(2,1)S(1)} async-done(((bf16[8,2,65536]{2,1,0:T(2,128)(2,1)}), bf16[8,2,65536]{2,1,0:T(2,128)(2,1)S(1)}, u32[]{:S(2)}, u32[]{:S(2)}) %all-to-all-start.1) | async-done | bytes 2097184 | tf_op jit(solution)/shard_map/all_to_all | solution.py:258
  115.4 4.4 %reshape.164 = bf16[8,1,131072]{2,1,0:T(2,128)(2,1)} reshape(bf16[8,2,65536]{2,1,0:T(2,128)(2,1)S(1)} %all-to-all-done.1) | data formatting | bytes 4194304
  119.9 4.7 %convolution_convert_fusion.1 = bf16[4,131072]{1,0:T(4,128)(2,1)S(1)} fusion(bf16[8,1,131072]{2,1,0:T(2,128)(2,1)} %reshape.164, s32[8]{0:T(128)S(1)} %reduce.2), kind=kOutput, calls=%fused_computation.2 | convolution fusion | flops 8912928 | bytes 3145760 | tf_op jit(solution)/shard_map/dot_general | solution.py:270
  124.6 1.3 copy.61
  125.8 5.0 %all-gather.3.cloned.1.call-done = bf16[8,512,1024]{2,1,0:T(8,128)(2,1)} async-done(((bf16[2,512,1024]{2,1,0:T(8,128)(2,1)}), bf16[8,512,1024]{2,1,0:T(8,128)(2,1)}) %all-gather.3.cloned.1.call-update) | async-done | bytes 8388624 | tf_op jit(solution)/shard_map/all_gather | solution.py:219
  130.8 24.6 %long_flash.1 = bf16[512,1024]{1,0:T(8,128)(2,1)} custom-call(s32[2]{0:T(128)} %pad_add_fusion.refs_0_, bf16[512,1024]{1,0:T(8,128)(2,1)} %bitcast.64, bf16[16,256,1024]{2,1,0:T(8,128)(2,1)} %bitcast.60, bf16[16,256,1024]{2,1,0:T(8,128)(2,1)} %bitcast.61), custom_call_target="tpu_custom_call" | custom-call | flops 4563402752 | bytes 11010048 | tf_op jit(solution)/shard_map/long_flash/pallas_call | solution.py:178
  (31 shorter events, 1.8 us)
Async XLA Ops:
  7.2 40.7 %copy-start = (s32[1,8]{1,0:T(1,128)S(1)}, s32[1,8]{1,0:T(1,128)}, u32[]{:S(2)}) copy-start(s32[1,8]{1,0:T(1,128)} %param.13) | copy-start | bytes 100
  7.2 123.7 %all-gather.3.cloned.1.call-start = ((), (), s32[]{:S(2)}) async-start(), calls=%async_computation.2 | async-start | bytes 10485760 | tf_op jit(solution)/shard_map/all_gather | solution.py:219
  8.6 22.1 %collective-permute-start = (bf16[512,1024]{1,0:T(8,128)(2,1)S(1)}, bf16[512,1024]{1,0:T(8,128)(2,1)S(1)}, u32[]{:S(2)}, u32[]{:S(2)}) collective-permute-start(bf16[512,1024]{1,0:T(8,128)(2,1)S(1)} %get-tuple-element.16), channel_id=1, source_target_pairs={{0,32},{32,0},{1,33},{33,1},{2,34},{34,2},{3,35},{35,3},{4,36},{36... | collective-permute-start | bytes 3145736 | tf_op jit(solution)/shard_map/ppermute | solution.py:217
  32.2 0.7 copy-start.5
  32.2 0.8 copy-start.6
  33.8 26.3 %all-to-all-start = ((s32[8,1,1]{2,1,0:T(1,128)}), s32[8,1,1]{2,1,0:T(1,128)S(1)}, u32[]{:S(2)}, u32[]{:S(2)}) async-start(s32[8,1,1]{2,1,0:T(1,128)} %copy.36), calls=%async_computation | async-start | bytes 8192 | tf_op jit(solution)/shard_map/all_to_all | solution.py:265
  60.1 7.4 %copy-start.1 = (bf16[1,128,1024]{2,1,0:T(8,128)(2,1)S(1)}, bf16[1,128,1024]{2,1,0:T(8,128)(2,1)}, u32[]{:S(2)}) copy-start(bf16[1,128,1024]{2,1,0:T(8,128)(2,1)} %param.14) | copy-start | bytes 786436
  60.1 7.5 %copy-start.2 = (bf16[1,128,512]{2,1,0:T(8,128)(2,1)S(1)}, bf16[1,128,512]{2,1,0:T(8,128)(2,1)}, u32[]{:S(2)}) copy-start(bf16[1,128,512]{2,1,0:T(8,128)(2,1)} %param.15) | copy-start | bytes 393220
  60.1 7.6 %copy-start.3 = (bf16[1,128,512]{2,1,0:T(8,128)(2,1)S(1)}, bf16[1,128,512]{2,1,0:T(8,128)(2,1)}, u32[]{:S(2)}) copy-start(bf16[1,128,512]{2,1,0:T(8,128)(2,1)} %param.16) | copy-start | bytes 393220
  60.1 7.7 %copy-start.4 = (s32[1,1,128]{2,1,0:T(1,128)S(1)}, s32[1,1,128]{2,1,0:T(1,128)}, u32[]{:S(2)}) copy-start(s32[1,1,128]{2,1,0:T(1,128)} %param.17) | copy-start | bytes 1540
  60.1 55.3 %all-to-all-start.1 = ((bf16[8,2,65536]{2,1,0:T(2,128)(2,1)}), bf16[8,2,65536]{2,1,0:T(2,128)(2,1)S(1)}, u32[]{:S(2)}, u32[]{:S(2)}) async-start(bf16[8,2,65536]{2,1,0:T(2,128)(2,1)} %reshape.163), calls=%async_computation.1 | async-start | bytes 4194304 | tf_op jit(solution)/shard_map/all_to_all | solution.py:258
Sparse Core Ops, SparseCore 0:
  32.3 98.4 all-gather.2

commit v5 on v4

--- a/solution.py
+++ b/solution.py
@@ -215,8 +215,9 @@
 
     y_size = lax.axis_size("yl")
     partner = lax.ppermute(kv_rows, "yl", [(i, (i + 1) % y_size) for i in range(y_size)])
-    kv_pair = jnp.stack([kv_rows, partner])
-    kv_all = lax.all_gather(kv_pair, "xx", axis=0, tiled=False)
+    kv_own_row = lax.all_gather(kv_rows, "xx", axis=0, tiled=False)
+    kv_other_row = lax.all_gather(partner, "xx", axis=0, tiled=False)
+    kv_all = jnp.stack([kv_own_row, kv_other_row], axis=1)
     kv_all = kv_all.reshape(2 * SPAN, half_rows, kv_rows.shape[-1])
     info = jnp.stack([member, length]).astype(jnp.int32)
     long_out = long_attention(info, query_long[0], kv_all, half_rows)

time: 163 us -> 169 us (1.037)
  the two profiles are of different devices: /device:TPU:1 before, /device:TPU:262 now
where the time goes in v5:
time: 169 us
  waiting for transfers between devices  71.4 us (42%)
  Pallas kernels  25.7 us (15%)
  starting transfers between devices  17.9 us (11%)
  other arithmetic  16.3 us (10%)
  local copies, waits for them, and re-layouts  15.7 us (9%)
  between operations  14.2 us (8%)
  matrix products  7.61 us (5%)
    all_to_all x1, waiting for transfers between devices, per_device(): lax.all_to_all(outgoing.reshape(groups, capacity, PAGE * page_width), 'gr...  47.9 us
    pallas_call x1, Pallas kernels, long_attention(): pl.pallas_call(lambda *refs: flash_kernel(*refs, block=block), grid_spec=...  25.7 us
    ppermute x1, waiting for transfers between devices, per_device(): lax.ppermute(kv_rows, 'yl', [(i, (i + 1) % y_size) for i in range(y_size)])  23.5 us
    unnamed x22, local copies, waits for them, and re-layouts  11.6 us
    another operation x1, other arithmetic, per_device(): kv_all = jnp.stack([kv_own_row, kv_other_row], axis=1)  7.45 us
    all_to_all x1, starting transfers between devices, per_device(): lax.all_to_all(outgoing.reshape(groups, capacity, PAGE * page_width), 'gr...  7.2 us
    all_to_all x1, starting transfers between devices, per_device(): lax.all_to_all(out_slots.reshape(groups, capacity), 'grp', split_axis=0,...  7.1 us
    dot_general x1, matrix products, per_device(): jnp.dot(chooser.astype(jnp.bfloat16), incoming.reshape(groups * capacity,...  4.71 us
  transfers between devices with their start and end apart: 5, of which 2 were waited for; matrix products, arithmetic and copies ran while one was open for 17% of the time, Pallas kernels for 0%

profile of v5, /device:TPU:262, one launch (start us, length us, event | category | flops | bytes accessed | tf_op | source)
XLA Modules:
  0.0 168.8 jit_solution(11444380258380623287)
XLA Ops:
  7.2 2.3 %pad_maximum_fusion.1 = bf16[512,1024]{1,0:T(8,128)(2,1)} fusion(bf16[512,512]{1,0:T(8,128)(2,1)} %bitcast.71, bf16[512,512]{1,0:T(8,128)(2,1)} %bitcast.72), kind=kLoop, calls=%fused_computation.13 | loop fusion | flops 2097152 | bytes 2097152 | tf_op jit(solution)/shard_map/concatenate | solution.py:214
  9.6 3.5 %collective-permute-start = (bf16[512,1024]{1,0:T(8,128)(2,1)}, bf16[512,1024]{1,0:T(8,128)(2,1)S(1)}, u32[]{:S(2)}, u32[]{:S(2)}) collective-permute-start(bf16[512,1024]{1,0:T(8,128)(2,1)} %pad_maximum_fusion.1), channel_id=1, source_target_pairs={{0,32},{32,0},{1,33},{33,1},{2,34},{34,2},{3,35},{35,3},{4,36},{36... | collective-permute-start | bytes 3145736 | tf_op jit(solution)/shard_map/ppermute | solution.py:217
  13.1 23.5 %collective-permute-done = bf16[512,1024]{1,0:T(8,128)(2,1)S(1)} collective-permute-done((bf16[512,1024]{1,0:T(8,128)(2,1)}, bf16[512,1024]{1,0:T(8,128)(2,1)S(1)}, u32[]{:S(2)}, u32[]{:S(2)}) %collective-permute-start) | collective-permute-done | bytes 1048608 | tf_op jit(solution)/shard_map/ppermute | solution.py:217
  36.6 1.0 copy-done.1
  37.9 0.7 copy.44
  38.6 7.1 %all-to-all-start = ((s32[8,1,1]{2,1,0:T(1,128)}), s32[8,1,1]{2,1,0:T(1,128)S(1)}, u32[]{:S(2)}, u32[]{:S(2)}) async-start(s32[8,1,1]{2,1,0:T(1,128)} %copy.44), calls=%async_computation | async-start | bytes 8192 | tf_op jit(solution)/shard_map/all_to_all | solution.py:266
  45.7 2.0 %concatenate.13 = bf16[4,131072]{1,0:T(4,128)(2,1)S(1)} reshape(bf16[512,1024]{1,0:T(8,128)(2,1)} %pad_maximum_fusion.1) | data formatting | bytes 2097152 | tf_op jit(solution)/shard_map/concatenate | solution.py:214
  47.7 0.6 constant_dynamic-slice_fusion
  48.3 0.7 compare_reduce_fusion
  49.2 0.6 copy.54
  49.8 2.4 %fusion = bf16[8,1,131072]{2,0,1:T(8,128)(2,1)} fusion(pred[4,131072]{1,0:T(4,128)(4,1)S(1)} %bitcast.70, bf16[4,131072]{1,0:T(4,128)(2,1)S(1)} %concatenate.13, s32[4]{0:T(128)S(1)} %fusion.22), kind=kOutput, calls=%fused_computation.1 | convolution fusion | flops 9961504 | bytes 3670032 | tf_op jit(solution)/shard_map/dot_general | solution.py:254
  52.2 0.5 broadcast.72
  52.8 3.9 %reduce.5 = bf16[8,131072]{1,0:T(8,128)(2,1)S(1)} reduce(bf16[8,1,131072]{2,0,1:T(8,128)(2,1)} %fusion, bf16[]{:T(256)} %broadcast.72), dimensions={1}, to_apply=%copy.45.reduce_sub_computation | reduce | bytes 4194306 | tf_op jit(solution)/shard_map/reshape | solution.py:260
  56.7 3.2 %reshape.165 = bf16[8,2,65536]{2,1,0:T(2,128)(2,1)} reshape(bf16[8,131072]{1,0:T(8,128)(2,1)S(1)} %reduce.5) | data formatting | bytes 4194304
  59.9 7.2 %all-to-all-start.1 = ((bf16[8,2,65536]{2,1,0:T(2,128)(2,1)}), bf16[8,2,65536]{2,1,0:T(2,128)(2,1)S(1)}, u32[]{:S(2)}, u32[]{:S(2)}) async-start(bf16[8,2,65536]{2,1,0:T(2,128)(2,1)} %reshape.165), calls=%async_computation.1 | async-start | bytes 4194304 | tf_op jit(solution)/shard_map/all_to_all | solution.py:259
  68.0 0.3 fusion.5
  68.2 0.9 copy.46
  69.1 1.3 pad_add_fusion.refs_0_
  70.6 47.9 %all-to-all-done.1 = bf16[8,2,65536]{2,1,0:T(2,128)(2,1)S(1)} async-done(((bf16[8,2,65536]{2,1,0:T(2,128)(2,1)}), bf16[8,2,65536]{2,1,0:T(2,128)(2,1)S(1)}, u32[]{:S(2)}, u32[]{:S(2)}) %all-to-all-start.1) | async-done | bytes 2097184 | tf_op jit(solution)/shard_map/all_to_all | solution.py:259
  118.5 4.4 %reshape.166 = bf16[8,1,131072]{2,1,0:T(2,128)(2,1)} reshape(bf16[8,2,65536]{2,1,0:T(2,128)(2,1)S(1)} %all-to-all-done.1) | data formatting | bytes 4194304
  122.9 4.7 %convolution_convert_fusion.1 = bf16[4,131072]{1,0:T(4,128)(2,1)S(1)} fusion(bf16[8,1,131072]{2,1,0:T(2,128)(2,1)} %reshape.166, s32[8]{0:T(128)S(1)} %reduce.2), kind=kOutput, calls=%fused_computation.2 | convolution fusion | flops 8912928 | bytes 3145760 | tf_op jit(solution)/shard_map/dot_general | solution.py:271
  127.6 1.3 copy.69
  128.9 7.4 %pad_maximum_fusion = bf16[4,2,512,1024]{3,2,1,0:T(8,128)(2,1)} fusion(bf16[4,1,512,1024]{3,2,1,0:T(8,128)(2,1)} %bitcast.67, bf16[4,1,512,1024]{3,2,1,0:T(8,128)(2,1)} %bitcast.66), kind=kLoop, calls=%fused_computation.3 | loop fusion | flops 4194304 | bytes 16777216 | tf_op jit(solution)/shard_map/stack | solution.py:220
  136.3 25.7 %long_flash.1 = bf16[512,1024]{1,0:T(8,128)(2,1)} custom-call(s32[2]{0:T(128)} %pad_add_fusion.refs_0_, bf16[512,1024]{1,0:T(8,128)(2,1)} %bitcast.68, bf16[16,256,1024]{2,1,0:T(8,128)(2,1)} %bitcast.63, bf16[16,256,1024]{2,1,0:T(8,128)(2,1)} %bitcast.64), custom_call_target="tpu_custom_call" | custom-call | flops 4563402752 | bytes 11010048 | tf_op jit(solution)/shard_map/long_flash/pallas_call | solution.py:178
  (36 shorter events, 1.7 us)
Async XLA Ops:
  7.2 40.5 %copy-start = (s32[1,8]{1,0:T(1,128)S(1)}, s32[1,8]{1,0:T(1,128)}, u32[]{:S(2)}) copy-start(s32[1,8]{1,0:T(1,128)} %param.13) | copy-start | bytes 100
  7.2 30.4 %copy-start.6 = (s32[1,4]{1,0:T(1,128)S(1)}, s32[1,4]{1,0:T(1,128)}, u32[]{:S(2)}) copy-start(s32[1,4]{1,0:T(1,128)} %param.18) | copy-start | bytes 52
  7.2 30.6 %copy-start.7 = (s32[1,4]{1,0:T(1,128)S(1)}, s32[1,4]{1,0:T(1,128)}, u32[]{:S(2)}) copy-start(s32[1,4]{1,0:T(1,128)} %param.19) | copy-start | bytes 52
  7.2 121.6 %all-gather.5.cloned.1.call-start = ((), (), s32[]{:S(2)}) async-start(), calls=%async_computation.2 | async-start | bytes 5242880 | tf_op jit(solution)/shard_map/all_gather | solution.py:218
  9.6 119.3 %all-gather.7.cloned.1.call-start = ((), (), s32[]{:S(2)}) async-start(), calls=%async_computation.3 | async-start | bytes 5242880 | tf_op jit(solution)/shard_map/all_gather | solution.py:219
  9.6 27.0 %collective-permute-start = (bf16[512,1024]{1,0:T(8,128)(2,1)}, bf16[512,1024]{1,0:T(8,128)(2,1)S(1)}, u32[]{:S(2)}, u32[]{:S(2)}) collective-permute-start(bf16[512,1024]{1,0:T(8,128)(2,1)} %pad_maximum_fusion.1), channel_id=1, source_target_pairs={{0,32},{32,0},{1,33},{33,1},{2,34},{34,2},{3,35},{35,3},{4,36},{36... | collective-permute-start | bytes 3145736 | tf_op jit(solution)/shard_map/ppermute | solution.py:217
  36.6 1.0 copy-start.1
  38.6 21.3 %all-to-all-start = ((s32[8,1,1]{2,1,0:T(1,128)}), s32[8,1,1]{2,1,0:T(1,128)S(1)}, u32[]{:S(2)}, u32[]{:S(2)}) async-start(s32[8,1,1]{2,1,0:T(1,128)} %copy.44), calls=%async_computation | async-start | bytes 8192 | tf_op jit(solution)/shard_map/all_to_all | solution.py:266
  56.6 10.5 %copy-start.2 = (bf16[1,128,1024]{2,1,0:T(8,128)(2,1)S(1)}, bf16[1,128,1024]{2,1,0:T(8,128)(2,1)}, u32[]{:S(2)}) copy-start(bf16[1,128,1024]{2,1,0:T(8,128)(2,1)} %param.14) | copy-start | bytes 786436
  56.7 10.6 %copy-start.3 = (bf16[1,128,512]{2,1,0:T(8,128)(2,1)S(1)}, bf16[1,128,512]{2,1,0:T(8,128)(2,1)}, u32[]{:S(2)}) copy-start(bf16[1,128,512]{2,1,0:T(8,128)(2,1)} %param.15) | copy-start | bytes 393220
  56.7 10.7 %copy-start.4 = (bf16[1,128,512]{2,1,0:T(8,128)(2,1)S(1)}, bf16[1,128,512]{2,1,0:T(8,128)(2,1)}, u32[]{:S(2)}) copy-start(bf16[1,128,512]{2,1,0:T(8,128)(2,1)} %param.16) | copy-start | bytes 393220
  56.7 10.8 %copy-start.5 = (s32[1,1,128]{2,1,0:T(1,128)S(1)}, s32[1,1,128]{2,1,0:T(1,128)}, u32[]{:S(2)}) copy-start(s32[1,1,128]{2,1,0:T(1,128)} %param.17) | copy-start | bytes 1540
  59.9 58.6 %all-to-all-start.1 = ((bf16[8,2,65536]{2,1,0:T(2,128)(2,1)}), bf16[8,2,65536]{2,1,0:T(2,128)(2,1)S(1)}, u32[]{:S(2)}, u32[]{:S(2)}) async-start(bf16[8,2,65536]{2,1,0:T(2,128)(2,1)} %reshape.165), calls=%async_computation.1 | async-start | bytes 4194304 | tf_op jit(solution)/shard_map/all_to_all | solution.py:259
Sparse Core Ops, SparseCore 0:
  10.7 53.6 all-gather.4
  66.5 53.9 all-gather.6
